TPU v7x, 128 devices: a whole 4x4x4 slice. The times are simulated.
128 devices in a mesh: slab: 32 (over z, y, core), cross: 4 (over x).
Axes of the slice: x: 4, y: 4, z: 4, core: 2. Of those that a mesh axis runs over, the one named last changes fastest.
Arguments:
- state: float32 [5, 64, 4096], P(None, 'slab', 'cross'), may hold values from -1.2 to 1.2
- rhs: float32 [5, 64, 4096], P(None, 'slab', 'cross'), may hold values from -1.2 to 1.2
- dinv: float32 [5, 5, 64, 4096], P(None, None, 'slab', 'cross'), may hold values from -0.3 to 2.3, as said below
- lower_jac: float32 [5, 5, 64, 4096], P(None, None, 'slab', 'cross'), may hold values from -0.3 to 2.3
- upper_jac: float32 [5, 5, 64, 4096], P(None, None, 'slab', 'cross'), may hold values from -0.3 to 2.3
- owner: int32 [131072, 1], P(('slab', 'cross')), may hold values from 0 to 127; in each aligned block of 1024 rows (0 to 1023, 1024 to 2047, ...) at most 32 rows name the same one
- donor_block: int32 [131072], P(('slab', 'cross')), may hold values from 0 to 15
- offsets: int32 [8, 131072], P(None, ('slab', 'cross')), may hold values from 0 to 127
- weights: float32 [8, 131072], P(None, ('slab', 'cross')), may hold values from 0 to 1, as said below
- receptor_perm: int32 [128, 16], P(('slab', 'cross')), may hold values from 0 to 15, each once within a row
Outputs:
- update: float32 [5, 64, 4096], P(None, 'slab', 'cross')
Inputs may be any that keep to these rules, and one draw needn't show every extreme that they name: `dinv`: each is s (I + E) with s between 0.5 and 2 a cell and small E. `weights`: positive; the 8 weights of one fringe point sum to one. Among the 1024 fringe points of one device no owner is named more than 32 times.
All inputs are finite; a program needn't handle non-finite values.
Results may differ from a plain program's by a relative error of at most 0.00021.
Values sent between devices are 32-bit elements; how exact they have to be, the bound alone decides.
No kernel may reach another device: no remote copies, remote signals or barrier semaphores. Data moves between devices by JAX's collectives and lax.ppermute only.
A program may use at most 64 MiB of HBM per device.

v0:
```python
import jax
import jax.numpy as jnp
from jax import lax
from jax.sharding import PartitionSpec as P

BLOCK_CELLS = 128
HIGHEST = lax.Precision.HIGHEST


def apply_block(matrix, vector):
    return jnp.sum(matrix * vector[None], axis=1)


def chain_blocks(later, earlier):
    return jnp.sum(later[:, :, None] * earlier[None], axis=1)


def interpolate_at_owner(state_flat, request):
    width, resident = state_flat.shape
    blocks = resident // BLOCK_CELLS
    corners = (request.shape[0] - 1) // 2
    block = request[0]
    offs = request[1 : 1 + corners]
    wts = request[1 + corners :]
    lanes = lax.broadcasted_iota(jnp.float32, (BLOCK_CELLS, 1), 0)
    spread = jnp.zeros((BLOCK_CELLS, request.shape[1]), jnp.float32)
    for k in range(corners):
        spread = spread + jnp.where(offs[k][None, :] == lanes, wts[k][None, :], 0.0)
    table = state_flat.reshape(width, blocks, BLOCK_CELLS).transpose(1, 0, 2)
    table = table.reshape(blocks * width, BLOCK_CELLS)
    every = jnp.dot(table, spread, precision=HIGHEST).reshape(blocks, width, -1)
    ids = lax.broadcasted_iota(jnp.float32, (blocks, 1, 1), 0)
    return jnp.sum(jnp.where(block[None, None, :] == ids, every, 0.0), axis=0)


def body(
    state, rhs, dinv, lower_jac, upper_jac, owner, donor_block, offsets, weights, receptor_perm
):
    width, planes, cells = state.shape
    resident_cells = planes * cells
    state_flat = state.reshape(width, resident_cells)
    devices = lax.axis_size(("slab", "cross"))
    slab_index = lax.axis_index("slab")
    fringe_rows = owner.shape[0]
    capacity = 4 * fringe_rows // devices
    blocks = resident_cells // BLOCK_CELLS
    square = width * width

    partial = []
    transfer = None
    for index in range(planes):
        step = chain_blocks(dinv[:, :, index], lower_jac[:, :, index])
        transfer = step if transfer is None else chain_blocks(step, transfer)
        partial.append(transfer)
    low_map = transfer
    up_steps = [chain_blocks(dinv[:, :, index], upper_jac[:, :, index]) for index in range(planes)]
    up_map = None
    response = partial[planes - 1]
    for index in range(planes - 1, -1, -1):
        up_map = up_steps[index] if up_map is None else chain_blocks(up_steps[index], up_map)
        if index < planes - 1:
            response = partial[index] + chain_blocks(up_steps[index], response)
    tile = (cells // BLOCK_CELLS, BLOCK_CELLS)
    maps = jnp.concatenate(
        [m.reshape((square,) + tile) for m in (low_map, up_map, response)], axis=0
    )
    all_maps = lax.all_gather(maps, "slab")
    peers = all_maps.shape[0]
    all_maps = all_maps.reshape((peers, 3, width, width) + tile)

    target = owner[:, 0]
    onehot = (target[:, None] == jnp.arange(devices, dtype=jnp.int32)[None, :]).astype(jnp.int32)
    slot = jnp.sum(jnp.cumsum(onehot, axis=0) * onehot, axis=1) - 1
    flat_slot = target * capacity + slot
    payload = jnp.concatenate(
        [donor_block[None, :].astype(jnp.float32), offsets.astype(jnp.float32), weights], axis=0
    )
    request = jnp.zeros((payload.shape[0], devices * capacity), jnp.float32)
    request = request.at[:, flat_slot].set(payload).reshape(-1, devices, capacity)
    received = lax.all_to_all(request, ("slab", "cross"), split_axis=1, concat_axis=1, tiled=True)
    answer = interpolate_at_owner(state_flat, received.reshape(received.shape[0], -1))
    answer = answer.reshape(width, devices, capacity)
    arrived = lax.all_to_all(answer, ("slab", "cross"), split_axis=1, concat_axis=1, tiled=True)
    interp = jnp.take(arrived.reshape(width, devices * capacity), flat_slot, axis=1)

    fringe_blocks = fringe_rows // BLOCK_CELLS
    chosen = receptor_perm[0, :fringe_blocks]
    hits = chosen[None, :] == jnp.arange(blocks, dtype=jnp.int32)[:, None]
    interp_blocks = interp.reshape(width, fringe_blocks, BLOCK_CELLS)
    placed = jnp.sum(
        jnp.where(hits[None, :, :, None], interp_blocks[:, None, :, :], 0.0), axis=2
    )
    state_blocks = state_flat.reshape(width, blocks, BLOCK_CELLS)
    rhs_blocks = rhs.reshape(width, blocks, BLOCK_CELLS)
    is_fringe = jnp.any(hits, axis=1)[None, :, None]
    forcing = jnp.where(is_fringe, placed - state_blocks, rhs_blocks)
    forcing = forcing.reshape(width, planes, cells)

    zero_lower = []
    value = jnp.zeros((width, cells), jnp.float32)
    for index in range(planes):
        value = apply_block(
            dinv[:, :, index], forcing[:, index] + apply_block(lower_jac[:, :, index], value)
        )
        zero_lower.append(value)
    value = jnp.zeros((width, cells), jnp.float32)
    for index in range(planes - 1, -1, -1):
        value = zero_lower[index] + apply_block(
            dinv[:, :, index], apply_block(upper_jac[:, :, index], value)
        )
    offsets_here = jnp.stack([zero_lower[planes - 1], value]).reshape((2, width) + tile)
    spread = jnp.broadcast_to(offsets_here[None], (peers,) + offsets_here.shape)
    every = lax.all_to_all(spread, "slab", 0, 0, tiled=True)

    entry = jnp.zeros((width,) + tile, jnp.float32)
    low_entry = entry
    up_offsets = []
    for at in range(peers):
        low_entry = jnp.where(at == slab_index, entry, low_entry)
        up_offsets.append(every[at, 1] + apply_block(all_maps[at, 2], entry))
        entry = apply_block(all_maps[at, 0], entry) + every[at, 0]
    entry = jnp.zeros((width,) + tile, jnp.float32)
    up_entry = entry
    for at in range(peers - 1, -1, -1):
        up_entry = jnp.where(at == slab_index, entry, up_entry)
        entry = apply_block(all_maps[at, 1], entry) + up_offsets[at]
    low_entry = low_entry.reshape(width, cells)
    up_entry = up_entry.reshape(width, cells)

    lower_planes = []
    value = low_entry
    for index in range(planes):
        value = apply_block(
            dinv[:, :, index], forcing[:, index] + apply_block(lower_jac[:, :, index], value)
        )
        lower_planes.append(value)
    result = [None] * planes
    value = up_entry
    for index in range(planes - 1, -1, -1):
        value = lower_planes[index] + apply_block(
            dinv[:, :, index], apply_block(upper_jac[:, :, index], value)
        )
        result[index] = value
    return jnp.stack(result, axis=1)


def solution(mesh):
    return jax.shard_map(
        body,
        mesh=mesh,
        in_specs=(
            P(None, "slab", "cross"),
            P(None, "slab", "cross"),
            P(None, None, "slab", "cross"),
            P(None, None, "slab", "cross"),
            P(None, None, "slab", "cross"),
            P(("slab", "cross"), None),
            P(("slab", "cross")),
            P(None, ("slab", "cross")),
            P(None, ("slab", "cross")),
            P(("slab", "cross"), None),
        ),
        out_specs=P(None, "slab", "cross"),
        check_vma=False,
    )
```

profile of v0, /device:TPU:0, one launch (start us, length us, event | category | flops | bytes accessed | tf_op | source)
XLA Modules:
  0.0 173.8 jit_solution(12341394977635561323)
XLA Ops:
  6.5 1.2 fusion.349
  7.7 1.2 fusion.348
  9.0 1.2 fusion.347
  13.2 3.6 %scatter_custom_fusion = f32[17,4096]{0,1:T(8,128)S(1)} fusion(s32[1024]{0:T(1024)S(1)} %bitcast.2135, f32[1024,17]{1,0:T(8,128)S(1)} %copy.77, f32[]{:T(128)} %constant.47.clone.1), kind=kCustom, calls=%fused_computation.44 | custom fusion | bytes 278532 | tf_op jit(solution)/shard_map/scatter | solution.py:79
  16.8 1.9 %copy.78 = f32[17,128,32]{2,0,1:T(8,128)} copy(f32[17,128,32]{0,2,1:T(8,128)S(1)} %bitcast.2030) | data formatting | bytes 557056 | tf_op jit(solution)/shard_map/reshape | solution.py:79
  18.7 2.8 %reshape.1676 = f32[128,1,544]{2,1,0:T(1,128)} reshape(f32[128,17,32]{2,1,0:T(8,128)} %bitcast.2031) | data formatting | bytes 557056
  21.5 11.4 %all-to-all-start = ((f32[128,1,544]{2,1,0:T(1,128)}), f32[128,1,544]{2,1,0:T(1,128)S(1)}, u32[]{:S(2)}, u32[]{:S(2)}) async-start(f32[128,1,544]{2,1,0:T(1,128)} %reshape.1676), calls=%async_computation | async-start | bytes 655360 | tf_op jit(solution)/shard_map/all_to_all | solution.py:80
  33.4 10.6 %all-to-all-done = f32[128,1,544]{2,1,0:T(1,128)S(1)} async-done(((f32[128,1,544]{2,1,0:T(1,128)}), f32[128,1,544]{2,1,0:T(1,128)S(1)}, u32[]{:S(2)}, u32[]{:S(2)}) %all-to-all-start) | async-done | bytes 278560 | tf_op jit(solution)/shard_map/all_to_all | solution.py:80
  44.5 1.4 reduce.72
  46.2 3.2 %slice_reduce_fusion.16 = (f32[128,32]{1,0:T(8,128)S(1)}, f32[128,32]{1,0:T(8,128)S(1)}, f32[128,32]{1,0:T(8,128)S(1)}, f32[128,32]{1,0:T(8,128)S(1)}, f32[128,3...) fusion(f32[17,128,32]{2,0,1:T(8,128)S(1)} %bitcast.2032), kind=kLoop, calls=%fused_computation.381 | loop fusion | bytes 557056 | tf_op jit(solution)/shard_map/slice | solution.py:22
  50.8 4.1 %convolution_bitcast_fusion = f32[80,4096]{1,0:T(8,128)} fusion(f32[80,128]{1,0:T(8,128)S(1)} %reshape.1561, f32[4096]{0:T(1024)S(1)} %broadcast_in_dim.158, f32[4096]{0:T(1024)S(1)} %eq.356, f32[4096]{0:T(1024)S(1)} %broadcast_in_dim.156, f32[4096]{0:T(1024)S(1)} %eq.352, f32[4096]{0:T(1024)S(1)} %broadcast_in_dim.154, f32[4096]{0:T(1024)S(1)} %eq.348, ...), kind=kOutput, calls=%fused_computation.2 | convolution fusion | flops 515375104 | bytes 1613824 | tf_op jit(solution)/shard_map/dot_general | solution.py:31
  54.9 1.5 reshape.1562
  58.2 4.8 %all-to-all-start.1 = ((f32[128,1,160]{2,1,0:T(1,128)}), f32[128,1,160]{2,1,0:T(1,128)S(1)}, u32[]{:S(2)}, u32[]{:S(2)}) async-start(f32[128,1,160]{2,1,0:T(1,128)} %reshape.1678), calls=%async_computation.1 | async-start | bytes 262144 | tf_op jit(solution)/shard_map/all_to_all | solution.py:83
  63.1 9.2 %all-to-all-done.1 = f32[128,1,160]{2,1,0:T(1,128)S(1)} async-done(((f32[128,1,160]{2,1,0:T(1,128)}), f32[128,1,160]{2,1,0:T(1,128)S(1)}, u32[]{:S(2)}, u32[]{:S(2)}) %all-to-all-start.1) | async-done | bytes 81952 | tf_op jit(solution)/shard_map/all_to_all | solution.py:83
  74.2 2.8 %gather_fusion = f32[1024,5]{1,0:T(8,128)S(1)} fusion(f32[5,4096]{0,1:T(8,128)S(1)} %bitcast.2033, s32[1024]{0:T(1024)S(1)} %broadcast_clamp_fusion), kind=kCustom, calls=%fused_computation | custom fusion | bytes 45056 | tf_op jit(solution)/shard_map/jit(_take)/gather | solution.py:84
  78.3 1.2 broadcast_in_dim.284
  79.4 4.0 %all-to-all-start.2 = ((f32[32,2,5,8,128]{4,3,2,1,0:T(8,128)}), f32[32,2,5,8,128]{4,3,2,1,0:T(8,128)S(1)}, u32[]{:S(2)}, u32[]{:S(2)}) async-start(f32[32,2,5,8,128]{4,3,2,1,0:T(8,128)} %broadcast_in_dim.284), calls=%async_computation.2 | async-start | bytes 2621440 | tf_op jit(solution)/shard_map/all_to_all | solution.py:113
  83.4 20.5 %all-to-all-done.2 = f32[32,2,5,8,128]{4,3,2,1,0:T(8,128)S(1)} async-done(((f32[32,2,5,8,128]{4,3,2,1,0:T(8,128)}), f32[32,2,5,8,128]{4,3,2,1,0:T(8,128)S(1)}, u32[]{:S(2)}, u32[]{:S(2)}) %all-to-all-start.2) | async-done | bytes 1310752 | tf_op jit(solution)/shard_map/all_to_all | solution.py:113
  106.1 1.0 fusion.41
  107.0 1.0 fusion.43
  110.0 1.0 fusion.49
  111.0 1.0 fusion.51
  113.9 1.0 fusion.57
  114.9 1.0 fusion.59
  117.9 1.0 fusion.65
  118.9 1.0 fusion.67
  121.8 1.0 fusion.73
  122.8 1.0 fusion.75
  125.8 1.0 fusion.81
  126.7 1.0 fusion.83
  130.7 1.0 fusion.91
  163.4 1.5 fusion.277
  (227 shorter events, 58.5 us)
Async XLA Ops:
  6.5 97.6 %all-gather.3.cloned.1.call-start = ((), (), s32[]{:S(2)}) async-start(), calls=%async_computation.3 | async-start | bytes 10137600 | tf_op jit(solution)/shard_map/all_gather | solution.py:67
  10.6 1.4 copy-start.2
  11.1 1.4 copy-start.3
  11.1 1.4 copy-start.5
  11.1 1.4 copy-start.4
  18.7 14.1 %copy-start.6 = (s32[1,16]{1,0:T(1,128)S(1)}, s32[1,16]{1,0:T(1,128)}, u32[]{:S(2)}) copy-start(s32[1,16]{1,0:T(1,128)} %param.19) | copy-start | bytes 196
  18.7 14.5 %copy-start = (f32[5,2,1024]{2,1,0:T(2,128)S(1)}, f32[5,2,1024]{2,1,0:T(2,128)}, u32[]{:S(2)}) copy-start(f32[5,2,1024]{2,1,0:T(2,128)} %param.10) | copy-start | bytes 122884
  21.5 22.5 %all-to-all-start = ((f32[128,1,544]{2,1,0:T(1,128)}), f32[128,1,544]{2,1,0:T(1,128)S(1)}, u32[]{:S(2)}, u32[]{:S(2)}) async-start(f32[128,1,544]{2,1,0:T(1,128)} %reshape.1676), calls=%async_computation | async-start | bytes 655360 | tf_op jit(solution)/shard_map/all_to_all | solution.py:80
  58.2 14.1 %all-to-all-start.1 = ((f32[128,1,160]{2,1,0:T(1,128)}), f32[128,1,160]{2,1,0:T(1,128)S(1)}, u32[]{:S(2)}, u32[]{:S(2)}) async-start(f32[128,1,160]{2,1,0:T(1,128)} %reshape.1678), calls=%async_computation.1 | async-start | bytes 262144 | tf_op jit(solution)/shard_map/all_to_all | solution.py:83
  73.4 4.3 %copy-start.1 = (f32[5,2,1024]{2,1,0:T(2,128)S(1)}, f32[5,2,1024]{2,1,0:T(2,128)}, u32[]{:S(2)}) copy-start(f32[5,2,1024]{2,1,0:T(2,128)} %param.11) | copy-start | bytes 122884
  79.4 24.5 %all-to-all-start.2 = ((f32[32,2,5,8,128]{4,3,2,1,0:T(8,128)}), f32[32,2,5,8,128]{4,3,2,1,0:T(8,128)S(1)}, u32[]{:S(2)}, u32[]{:S(2)}) async-start(f32[32,2,5,8,128]{4,3,2,1,0:T(8,128)} %broadcast_in_dim.284), calls=%async_computation.2 | async-start | bytes 2621440 | tf_op jit(solution)/shard_map/all_to_all | solution.py:113
Sparse Core Ops, SparseCore 0:
  12.1 62.6 all-gather.2
where the time goes:
time: 176 us; the launch traced here: 174 us
  other arithmetic  67.5 us (38%)
  waiting for transfers between devices  40.3 us (23%)
  local copies, waits for them, and re-layouts  27.1 us (15%)
  starting transfers between devices  20.1 us (11%)
  between operations  14.7 us (8%)
  matrix products  4.15 us (2%)
    reduce_sum x76, other arithmetic, apply_block(): return jnp.sum(matrix * vector[None], axis=1)  59.3 us
    all_to_all x1, waiting for transfers between devices, body(): every = lax.all_to_all(spread, 'slab', 0, 0, tiled=True)  20.5 us
    all_to_all x1, starting transfers between devices, body(): lax.all_to_all(request, ('slab', 'cross'), split_axis=1, concat_axis=1, t...  11.4 us
    all_to_all x1, waiting for transfers between devices, body(): lax.all_to_all(request, ('slab', 'cross'), split_axis=1, concat_axis=1, t...  10.6 us
    all_to_all x1, waiting for transfers between devices, body(): lax.all_to_all(answer, ('slab', 'cross'), split_axis=1, concat_axis=1, ti...  9.18 us
    all_to_all x1, starting transfers between devices, body(): lax.all_to_all(answer, ('slab', 'cross'), split_axis=1, concat_axis=1, ti...  4.8 us
    unnamed x24, local copies, waits for them, and re-layouts  4.35 us
    dot_general x1, matrix products, interpolate_at_owner(): every = jnp.dot(table, spread, precision=HIGHEST).reshape(blocks, width, -1)  4.15 us
  transfers between devices with their start and end apart: 4, of which 3 were waited for; matrix products, arithmetic and copies ran while one was open for 18% of the time, Pallas kernels for 0%

commit v1 on v0

--- a/solution.py
+++ b/solution.py
@@ -1,6 +1,8 @@
 import jax
 import jax.numpy as jnp
 from jax import lax
+from jax.experimental import pallas as pl
+from jax.experimental.pallas import tpu as pltpu
 from jax.sharding import PartitionSpec as P
 
 BLOCK_CELLS = 128
@@ -31,6 +33,69 @@
     every = jnp.dot(table, spread, precision=HIGHEST).reshape(blocks, width, -1)
     ids = lax.broadcasted_iota(jnp.float32, (blocks, 1, 1), 0)
     return jnp.sum(jnp.where(block[None, None, :] == ids, every, 0.0), axis=0)
+
+
+def fold_kernel(index_ref, maps_ref, offsets_ref, out_ref, up_ref):
+    peers = maps_ref.shape[0]
+    width = out_ref.shape[1]
+    square = width * width
+    here = index_ref[0]
+    zero = offsets_ref[0, 0] * 0.0
+
+    def matvec(at, base, vector):
+        rows = []
+        for i in range(width):
+            total = maps_ref[at, base + i * width] * vector[0]
+            for j in range(1, width):
+                total = total + maps_ref[at, base + i * width + j] * vector[j]
+            rows.append(total)
+        return rows
+
+    def lower_step(at, carry):
+        entry, kept = carry
+        hit = at == here
+        kept = tuple(jnp.where(hit, e, k) for e, k in zip(entry, kept))
+        response = matvec(at, 2 * square, entry)
+        for i in range(width):
+            up_ref[at, i] = offsets_ref[at, width + i] + response[i]
+        moved = matvec(at, 0, entry)
+        entry = tuple(moved[i] + offsets_ref[at, i] for i in range(width))
+        return entry, kept
+
+    start = (tuple([zero] * width), tuple([zero] * width))
+    _, low = lax.fori_loop(0, peers, lower_step, start)
+
+    def upper_step(step, carry):
+        at = peers - 1 - step
+        entry, kept = carry
+        hit = at == here
+        kept = tuple(jnp.where(hit, e, k) for e, k in zip(entry, kept))
+        moved = matvec(at, square, entry)
+        entry = tuple(moved[i] + up_ref[at, i] for i in range(width))
+        return entry, kept
+
+    _, up = lax.fori_loop(0, peers, upper_step, start)
+    for i in range(width):
+        out_ref[0, i] = low[i]
+        out_ref[1, i] = up[i]
+
+
+def fold_entries(index, all_maps, every):
+    peers, _, sub, lanes = all_maps.shape
+    width = every.shape[1] // 2
+    vmem = pltpu.MemorySpace.VMEM
+    return pl.pallas_call(
+        fold_kernel,
+        out_shape=jax.ShapeDtypeStruct((2, width, sub, lanes), jnp.float32),
+        in_specs=[
+            pl.BlockSpec(memory_space=pltpu.MemorySpace.SMEM),
+            pl.BlockSpec(memory_space=vmem),
+            pl.BlockSpec(memory_space=vmem),
+        ],
+        out_specs=pl.BlockSpec(memory_space=vmem),
+        scratch_shapes=[pltpu.VMEM((peers, width, sub, lanes), jnp.float32)],
+        compiler_params=pltpu.CompilerParams(vmem_limit_bytes=48 * 1024 * 1024),
+    )(index, all_maps, every)
 
 
 def body(
@@ -66,7 +131,6 @@
     )
     all_maps = lax.all_gather(maps, "slab")
     peers = all_maps.shape[0]
-    all_maps = all_maps.reshape((peers, 3, width, width) + tile)
 
     target = owner[:, 0]
     onehot = (target[:, None] == jnp.arange(devices, dtype=jnp.int32)[None, :]).astype(jnp.int32)
@@ -112,20 +176,11 @@
     spread = jnp.broadcast_to(offsets_here[None], (peers,) + offsets_here.shape)
     every = lax.all_to_all(spread, "slab", 0, 0, tiled=True)
 
-    entry = jnp.zeros((width,) + tile, jnp.float32)
-    low_entry = entry
-    up_offsets = []
-    for at in range(peers):
-        low_entry = jnp.where(at == slab_index, entry, low_entry)
-        up_offsets.append(every[at, 1] + apply_block(all_maps[at, 2], entry))
-        entry = apply_block(all_maps[at, 0], entry) + every[at, 0]
-    entry = jnp.zeros((width,) + tile, jnp.float32)
-    up_entry = entry
-    for at in range(peers - 1, -1, -1):
-        up_entry = jnp.where(at == slab_index, entry, up_entry)
-        entry = apply_block(all_maps[at, 1], entry) + up_offsets[at]
-    low_entry = low_entry.reshape(width, cells)
-    up_entry = up_entry.reshape(width, cells)
+    every = every.reshape((peers, 2 * width) + tile)
+    index = jnp.reshape(slab_index, (1,)).astype(jnp.int32)
+    entries = fold_entries(index, all_maps, every).reshape(2, width, cells)
+    low_entry = entries[0]
+    up_entry = entries[1]
 
     lower_planes = []
     value = low_entry

time: 176 us -> 118 us (0.67)
  other arithmetic: 67.5 us -> 6.5 us
  Pallas kernels: 0 us -> 4.95 us
    reduce_sum x76 -> x14, other arithmetic: 59.3 us -> 1.06 us  [apply_block(): return jnp.sum(matrix * vector[None], axis=1)]
    pallas_call x0 -> x1, Pallas kernels: none -> 4.95 us  [fold_entries(): pl.pallas_call(fold_kernel, out_shape=jax.ShapeDtypeStruct((2, width, sub...]
    select_n x2 -> x0, other arithmetic: 2.29 us -> none  [the longest x1 1.46 us: body(): up_entry = jnp.where(at == slab_index, entry, up_entry)]
    unnamed x24 -> x23, local copies, waits for them, and re-layouts: 4.35 us -> 4.27 us
  transfers between devices with their start and end apart: 4 -> 4, of which waited for: 3 -> 3; matrix products, arithmetic and copies ran while one was open for 18% -> 27% of each run, Pallas kernels for 0% -> 0%
where the time goes in v1:
time: 118 us; the launch traced here: 117 us
  waiting for transfers between devices  40.3 us (34%)
  local copies, waits for them, and re-layouts  27 us (23%)
  starting transfers between devices  20.1 us (17%)
  between operations  14 us (12%)
  other arithmetic  6.5 us (6%)
  Pallas kernels  4.95 us (4%)
  matrix products  4.15 us (4%)
    all_to_all x1, waiting for transfers between devices, body(): every = lax.all_to_all(spread, 'slab', 0, 0, tiled=True)  20.6 us
    all_to_all x1, starting transfers between devices, body(): lax.all_to_all(request, ('slab', 'cross'), split_axis=1, concat_axis=1, t...  11.4 us
    all_to_all x1, waiting for transfers between devices, body(): lax.all_to_all(request, ('slab', 'cross'), split_axis=1, concat_axis=1, t...  10.6 us
    all_to_all x1, waiting for transfers between devices, body(): lax.all_to_all(answer, ('slab', 'cross'), split_axis=1, concat_axis=1, ti...  9.18 us
    pallas_call x1, Pallas kernels, fold_entries(): pl.pallas_call(fold_kernel, out_shape=jax.ShapeDtypeStruct((2, width, sub...  4.95 us
    all_to_all x1, starting transfers between devices, body(): lax.all_to_all(answer, ('slab', 'cross'), split_axis=1, concat_axis=1, ti...  4.81 us
    unnamed x23, local copies, waits for them, and re-layouts  4.27 us
    dot_general x1, matrix products, interpolate_at_owner(): every = jnp.dot(table, spread, precision=HIGHEST).reshape(blocks, width, -1)  4.15 us
  transfers between devices with their start and end apart: 4, of which 3 were waited for; matrix products, arithmetic and copies ran while one was open for 27% of the time, Pallas kernels for 0%

profile of v1, /device:TPU:0, one launch (start us, length us, event | category | flops | bytes accessed | tf_op | source)
XLA Modules:
  0.0 117.1 jit_solution(489226726511817957)
XLA Ops:
  6.5 1.2 %fusion.40 = (f32[5,5,1,1024]{3,2,1,0:T(1,128)S(1)}, f32[5,5,1,1024]{3,2,1,0:T(1,128)S(1)}) fusion(f32[5,5,2,1024]{3,2,1,0:T(2,128)} %param.13), kind=kLoop, calls=%fused_computation.132 | loop fusion | bytes 409600 | tf_op jit(solution)/shard_map/slice | solution.py:117
  7.7 1.2 %fusion.42 = (f32[5,5,1,1024]{3,2,1,0:T(1,128)S(1)}, f32[5,5,1,1024]{3,2,1,0:T(1,128)S(1)}) fusion(f32[5,5,2,1024]{3,2,1,0:T(2,128)} %param.12), kind=kLoop, calls=%fused_computation.134 | loop fusion | bytes 409600 | tf_op jit(solution)/shard_map/slice | solution.py:189
  9.0 1.2 %fusion.41 = (f32[5,5,1,1024]{3,2,1,0:T(1,128)S(1)}, f32[5,5,1,1024]{3,2,1,0:T(1,128)S(1)}) fusion(f32[5,5,2,1024]{3,2,1,0:T(2,128)} %param.14), kind=kLoop, calls=%fused_computation.133 | loop fusion | bytes 409600 | tf_op jit(solution)/shard_map/slice | solution.py:121
  11.2 0.7 pad_maximum_fusion
  12.0 0.2 fusion.35
  12.5 0.2 copy.77
  12.7 0.4 fusion.34
  13.2 3.6 %scatter_custom_fusion = f32[17,4096]{0,1:T(8,128)S(1)} fusion(s32[1024]{0:T(1024)S(1)} %bitcast.135, f32[1024,17]{1,0:T(8,128)S(1)} %copy.77, f32[]{:T(128)} %constant.36.clone.1), kind=kCustom, calls=%fused_computation.44 | custom fusion | bytes 278532 | tf_op jit(solution)/shard_map/scatter | solution.py:143
  16.8 1.9 %copy.78 = f32[17,128,32]{2,0,1:T(8,128)} copy(f32[17,128,32]{0,2,1:T(8,128)S(1)} %bitcast.121) | data formatting | bytes 557056 | tf_op jit(solution)/shard_map/reshape | solution.py:143
  18.7 2.8 %reshape.388 = f32[128,1,544]{2,1,0:T(1,128)} reshape(f32[128,17,32]{2,1,0:T(8,128)} %bitcast.122) | data formatting | bytes 557056
  21.5 11.4 %all-to-all-start = ((f32[128,1,544]{2,1,0:T(1,128)}), f32[128,1,544]{2,1,0:T(1,128)S(1)}, u32[]{:S(2)}, u32[]{:S(2)}) async-start(f32[128,1,544]{2,1,0:T(1,128)} %reshape.388), calls=%async_computation | async-start | bytes 655360 | tf_op jit(solution)/shard_map/all_to_all | solution.py:144
  33.4 10.6 %all-to-all-done = f32[128,1,544]{2,1,0:T(1,128)S(1)} async-done(((f32[128,1,544]{2,1,0:T(1,128)}), f32[128,1,544]{2,1,0:T(1,128)S(1)}, u32[]{:S(2)}, u32[]{:S(2)}) %all-to-all-start) | async-done | bytes 278560 | tf_op jit(solution)/shard_map/all_to_all | solution.py:144
  44.0 0.5 broadcast.154
  44.5 1.4 %reduce.70 = f32[128,544]{1,0:T(8,128)S(1)} reduce(f32[128,1,544]{2,1,0:T(1,128)S(1)} %all-to-all-done, f32[]{:T(128)} %broadcast.154), dimensions={1}, to_apply=%all_to_all.9.reduce_sub_computation | reduce | bytes 557060 | tf_op jit(solution)/shard_map/all_to_all | solution.py:144
  45.9 0.3 reshape.389
  46.2 3.2 %slice_reduce_fusion.16 = (f32[128,32]{1,0:T(8,128)S(1)}, f32[128,32]{1,0:T(8,128)S(1)}, f32[128,32]{1,0:T(8,128)S(1)}, f32[128,32]{1,0:T(8,128)S(1)}, f32[128,3...) fusion(f32[17,128,32]{2,0,1:T(8,128)S(1)} %bitcast.123), kind=kLoop, calls=%fused_computation.104 | loop fusion | bytes 557056 | tf_op jit(solution)/shard_map/slice | solution.py:24
  50.8 4.1 %convolution_bitcast_fusion = f32[80,4096]{1,0:T(8,128)} fusion(f32[80,128]{1,0:T(8,128)S(1)} %reshape.273, f32[4096]{0:T(1024)S(1)} %broadcast_in_dim.186, f32[4096]{0:T(1024)S(1)} %eq.228, f32[4096]{0:T(1024)S(1)} %broadcast_in_dim.184, f32[4096]{0:T(1024)S(1)} %eq.224, f32[4096]{0:T(1024)S(1)} %broadcast_in_dim.182, f32[4096]{0:T(1024)S(1)} %eq.220, ...), kind=kOutput, calls=%fused_computation.2 | convolution fusion | flops 515375104 | bytes 1613824 | tf_op jit(solution)/shard_map/dot_general | solution.py:33
  54.9 1.5 %reshape.274 = f32[16,5,4096]{2,1,0:T(8,128)S(1)} reshape(f32[80,4096]{1,0:T(8,128)} %convolution_bitcast_fusion) | data formatting | bytes 2621440 | tf_op jit(solution)/shard_map/reshape | solution.py:33
  56.6 0.4 select_reduce_fusion
  57.1 0.2 copy.155
  57.3 0.9 reshape.390
  58.2 4.8 %all-to-all-start.1 = ((f32[128,1,160]{2,1,0:T(1,128)}), f32[128,1,160]{2,1,0:T(1,128)S(1)}, u32[]{:S(2)}, u32[]{:S(2)}) async-start(f32[128,1,160]{2,1,0:T(1,128)} %reshape.390), calls=%async_computation.1 | async-start | bytes 262144 | tf_op jit(solution)/shard_map/all_to_all | solution.py:147
  63.1 9.2 %all-to-all-done.1 = f32[128,1,160]{2,1,0:T(1,128)S(1)} async-done(((f32[128,1,160]{2,1,0:T(1,128)}), f32[128,1,160]{2,1,0:T(1,128)S(1)}, u32[]{:S(2)}, u32[]{:S(2)}) %all-to-all-start.1) | async-done | bytes 81952 | tf_op jit(solution)/shard_map/all_to_all | solution.py:147
  72.3 1.0 reduce.71
  73.4 0.8 copy.81
  74.2 2.8 %gather_fusion = f32[1024,5]{1,0:T(8,128)S(1)} fusion(f32[5,4096]{0,1:T(8,128)S(1)} %bitcast.124, s32[1024]{0:T(1024)S(1)} %broadcast_clamp_fusion), kind=kCustom, calls=%fused_computation | custom fusion | bytes 45056 | tf_op jit(solution)/shard_map/jit(_take)/gather | solution.py:148
  77.0 0.2 broadcast_select_fusion
  78.3 1.2 broadcast_in_dim.193
  79.4 4.0 %all-to-all-start.2 = ((f32[32,2,5,8,128]{4,3,2,1,0:T(8,128)}), f32[32,2,5,8,128]{4,3,2,1,0:T(8,128)S(1)}, u32[]{:S(2)}, u32[]{:S(2)}) async-start(f32[32,2,5,8,128]{4,3,2,1,0:T(8,128)} %broadcast_in_dim.193), calls=%async_computation.2 | async-start | bytes 2621440 | tf_op jit(solution)/shard_map/all_to_all | solution.py:177
  83.4 20.6 %all-to-all-done.2 = f32[32,2,5,8,128]{4,3,2,1,0:T(8,128)S(1)} async-done(((f32[32,2,5,8,128]{4,3,2,1,0:T(8,128)}), f32[32,2,5,8,128]{4,3,2,1,0:T(8,128)S(1)}, u32[]{:S(2)}, u32[]{:S(2)}) %all-to-all-start.2) | async-done | bytes 1310752 | tf_op jit(solution)/shard_map/all_to_all | solution.py:177
  103.9 5.0 %shard_map.100 = f32[2,5,8,128]{3,2,1,0:T(8,128)S(1)} custom-call(s32[1]{0:T(128)} %bitcast.18.index_ref, f32[32,75,8,128]{3,2,1,0:T(8,128)} %bitcast.120, f32[32,10,8,128]{3,2,1,0:T(8,128)S(1)} %bitcast.119), custom_call_target="tpu_custom_call" | custom-call | tf_op jit(solution)/shard_map/pallas_call | solution.py:87
  109.6 0.7 copy.88
  (102 shorter events, 5.0 us)
Async XLA Ops:
  6.5 97.4 %all-gather.3.cloned.1.call-start = ((), (), s32[]{:S(2)}) async-start(), calls=%async_computation.3 | async-start | bytes 10137600 | tf_op jit(solution)/shard_map/all_gather | solution.py:132
  10.6 1.4 %copy-start.2 = (s32[1024,1]{0,1:T(1,128)S(1)}, s32[1024,1]{0,1:T(1,128)}, u32[]{:S(2)}) copy-start(s32[1024,1]{0,1:T(1,128)} %param.15) | copy-start | bytes 12292
  11.1 1.4 %copy-start.3 = (s32[8,1024]{1,0:T(8,128)S(1)}, s32[8,1024]{1,0:T(8,128)}, u32[]{:S(2)}) copy-start(s32[8,1024]{1,0:T(8,128)} %param.17) | copy-start | bytes 98308
  11.1 1.4 %copy-start.5 = (s32[1024]{0:T(1024)S(1)}, s32[1024]{0:T(1024)}, u32[]{:S(2)}) copy-start(s32[1024]{0:T(1024)} %param.16) | copy-start | bytes 12292
  11.1 1.4 %copy-start.4 = (f32[8,1024]{1,0:T(8,128)S(1)}, f32[8,1024]{1,0:T(8,128)}, u32[]{:S(2)}) copy-start(f32[8,1024]{1,0:T(8,128)} %param.18) | copy-start | bytes 98308
  18.7 14.1 %copy-start.6 = (s32[1,16]{1,0:T(1,128)S(1)}, s32[1,16]{1,0:T(1,128)}, u32[]{:S(2)}) copy-start(s32[1,16]{1,0:T(1,128)} %param.19) | copy-start | bytes 196
  18.7 14.5 %copy-start = (f32[5,2,1024]{2,1,0:T(2,128)S(1)}, f32[5,2,1024]{2,1,0:T(2,128)}, u32[]{:S(2)}) copy-start(f32[5,2,1024]{2,1,0:T(2,128)} %param.10) | copy-start | bytes 122884
  21.5 22.5 %all-to-all-start = ((f32[128,1,544]{2,1,0:T(1,128)}), f32[128,1,544]{2,1,0:T(1,128)S(1)}, u32[]{:S(2)}, u32[]{:S(2)}) async-start(f32[128,1,544]{2,1,0:T(1,128)} %reshape.388), calls=%async_computation | async-start | bytes 655360 | tf_op jit(solution)/shard_map/all_to_all | solution.py:144
  58.2 14.1 %all-to-all-start.1 = ((f32[128,1,160]{2,1,0:T(1,128)}), f32[128,1,160]{2,1,0:T(1,128)S(1)}, u32[]{:S(2)}, u32[]{:S(2)}) async-start(f32[128,1,160]{2,1,0:T(1,128)} %reshape.390), calls=%async_computation.1 | async-start | bytes 262144 | tf_op jit(solution)/shard_map/all_to_all | solution.py:147
  73.4 4.3 %copy-start.1 = (f32[5,2,1024]{2,1,0:T(2,128)S(1)}, f32[5,2,1024]{2,1,0:T(2,128)}, u32[]{:S(2)}) copy-start(f32[5,2,1024]{2,1,0:T(2,128)} %param.11) | copy-start | bytes 122884
  79.4 24.5 %all-to-all-start.2 = ((f32[32,2,5,8,128]{4,3,2,1,0:T(8,128)}), f32[32,2,5,8,128]{4,3,2,1,0:T(8,128)S(1)}, u32[]{:S(2)}, u32[]{:S(2)}) async-start(f32[32,2,5,8,128]{4,3,2,1,0:T(8,128)} %broadcast_in_dim.193), calls=%async_computation.2 | async-start | bytes 2621440 | tf_op jit(solution)/shard_map/all_to_all | solution.py:177
Sparse Core Ops, SparseCore 0:
  12.1 62.6 all-gather.2

commit v2 on v1

--- a/solution.py
+++ b/solution.py
@@ -30,7 +30,7 @@
         spread = spread + jnp.where(offs[k][None, :] == lanes, wts[k][None, :], 0.0)
     table = state_flat.reshape(width, blocks, BLOCK_CELLS).transpose(1, 0, 2)
     table = table.reshape(blocks * width, BLOCK_CELLS)
-    every = jnp.dot(table, spread, precision=HIGHEST).reshape(blocks, width, -1)
+    every = jnp.dot(table, spread, precision=lax.Precision.HIGH).reshape(blocks, width, -1)
     ids = lax.broadcasted_iota(jnp.float32, (blocks, 1, 1), 0)
     return jnp.sum(jnp.where(block[None, None, :] == ids, every, 0.0), axis=0)
 
@@ -139,10 +139,13 @@
     payload = jnp.concatenate(
         [donor_block[None, :].astype(jnp.float32), offsets.astype(jnp.float32), weights], axis=0
     )
-    request = jnp.zeros((payload.shape[0], devices * capacity), jnp.float32)
-    request = request.at[:, flat_slot].set(payload).reshape(-1, devices, capacity)
-    received = lax.all_to_all(request, ("slab", "cross"), split_axis=1, concat_axis=1, tiled=True)
-    answer = interpolate_at_owner(state_flat, received.reshape(received.shape[0], -1))
+    rows = payload.shape[0]
+    columns = jnp.arange(rows, dtype=jnp.int32)[None, :] * capacity + slot[:, None]
+    request = jnp.zeros((devices, rows * capacity), jnp.float32)
+    request = request.at[target[:, None], columns].set(payload.T)
+    received = lax.all_to_all(request, ("slab", "cross"), split_axis=0, concat_axis=0, tiled=True)
+    received = received.reshape(devices, rows, capacity).transpose(1, 0, 2)
+    answer = interpolate_at_owner(state_flat, received.reshape(rows, devices * capacity))
     answer = answer.reshape(width, devices, capacity)
     arrived = lax.all_to_all(answer, ("slab", "cross"), split_axis=1, concat_axis=1, tiled=True)
     interp = jnp.take(arrived.reshape(width, devices * capacity), flat_slot, axis=1)

time: 118 us -> 172 us (1.46)
  local copies, waits for them, and re-layouts: 27 us -> 83 us
    unnamed x23 -> x28, local copies, waits for them, and re-layouts: 4.27 us -> 65.9 us
    scatter x1 -> x0, local copies, waits for them, and re-layouts: 3.59 us -> none  [body(): request.at[:, flat_slot].set(payload).reshape(-1, devices, capacity)]
    slice x1 -> x2, local copies, waits for them, and re-layouts: 3.23 us -> 0.12 us  [interpolate_at_owner(): block = request[0]]
    reshape x2 -> x1, local copies, waits for them, and re-layouts: 3.47 us -> 1.52 us  [interpolate_at_owner(): jnp.dot(table, spread, precision=lax.Precision.HIGH)]
  transfers between devices with their start and end apart: 4 -> 4, of which waited for: 3 -> 3; matrix products, arithmetic and copies ran while one was open for 27% -> 50% of each run, Pallas kernels for 0% -> 0%
where the time goes in v2:
time: 172 us
  local copies, waits for them, and re-layouts  83 us (48%)
  waiting for transfers between devices  40.5 us (24%)
  starting transfers between devices  19.9 us (12%)
  between operations  14.2 us (8%)
  other arithmetic  5.89 us (3%)
  Pallas kernels  4.95 us (3%)
  matrix products  3.43 us (2%)
    unnamed x28, local copies, waits for them, and re-layouts  65.9 us
    all_to_all x1, waiting for transfers between devices, body(): every = lax.all_to_all(spread, 'slab', 0, 0, tiled=True)  20.6 us
    all_to_all x1, starting transfers between devices, body(): lax.all_to_all(request, ('slab', 'cross'), split_axis=0, concat_axis=0, t...  11.2 us
    all_to_all x1, waiting for transfers between devices, body(): lax.all_to_all(request, ('slab', 'cross'), split_axis=0, concat_axis=0, t...  10.7 us
    all_to_all x1, waiting for transfers between devices, body(): lax.all_to_all(answer, ('slab', 'cross'), split_axis=1, concat_axis=1, ti...  9.21 us
    pallas_call x1, Pallas kernels, fold_entries(): pl.pallas_call(fold_kernel, out_shape=jax.ShapeDtypeStruct((2, width, sub...  4.95 us
    all_to_all x1, starting transfers between devices, body(): lax.all_to_all(answer, ('slab', 'cross'), split_axis=1, concat_axis=1, ti...  4.78 us
    all_to_all x1, starting transfers between devices, body(): every = lax.all_to_all(spread, 'slab', 0, 0, tiled=True)  3.95 us
  transfers between devices with their start and end apart: 4, of which 3 were waited for; matrix products, arithmetic and copies ran while one was open for 50% of the time, Pallas kernels for 0%

profile of v2, /device:TPU:0, one launch (start us, length us, event | category | flops | bytes accessed | tf_op | source)
XLA Modules:
  0.0 171.8 jit_solution(4459230834527882930)
XLA Ops:
  6.5 1.2 fusion.41
  7.7 1.2 fusion.43
  9.0 1.2 fusion.42
  11.1 0.8 pad_maximum_fusion
  12.1 0.2 fusion.33
  12.5 0.4 fusion.32
  13.1 0.3 multiply_reduce_fusion.23
  13.4 0.3 and_reduce_fusion
  13.8 0.2 copy.160
  14.0 0.3 reshape.357
  14.4 0.2 copy.161
  14.6 0.3 reshape.359
  15.0 64.1 %scatter_custom_fusion = f32[69632]{0:T(1024)S(1)} fusion(s32[17408]{0:T(1024)S(1)} %reshape.357, f32[17408]{0:T(1024)S(1)} %reshape.359, f32[]{:T(128)} %constant.19.clone.1), kind=kCustom, calls=%fused_computation.88 | custom fusion | bytes 278532
  79.1 0.9 copy.162
  80.0 11.2 %all-to-all-start = ((f32[128,1,544]{2,1,0:T(1,128)}), f32[128,1,544]{2,1,0:T(1,128)S(1)}, u32[]{:S(2)}, u32[]{:S(2)}) async-start(f32[128,1,544]{2,1,0:T(1,128)} %copy.162), calls=%async_computation | async-start | bytes 655360 | tf_op jit(solution)/shard_map/all_to_all | solution.py:146
  91.8 10.7 %all-to-all-done = f32[128,1,544]{2,1,0:T(1,128)S(1)} async-done(((f32[128,1,544]{2,1,0:T(1,128)}), f32[128,1,544]{2,1,0:T(1,128)S(1)}, u32[]{:S(2)}, u32[]{:S(2)}) %all-to-all-start) | async-done | bytes 278560 | tf_op jit(solution)/shard_map/all_to_all | solution.py:146
  105.6 3.4 %convolution_bitcast_fusion = f32[80,4096]{1,0:T(8,128)} fusion(f32[80,128]{1,0:T(8,128)S(1)} %reshape.337, f32[4096]{0:T(1024)S(1)} %broadcast_in_dim.194, f32[4096]{0:T(1024)S(1)} %eq.228, f32[4096]{0:T(1024)S(1)} %broadcast_in_dim.192, f32[4096]{0:T(1024)S(1)} %eq.224, f32[4096]{0:T(1024)S(1)} %broadcast_in_dim.190, f32[4096]{0:T(1024)S(1)} %eq.220, ...), kind=kOutput, calls=%fused_computation.2 | convolution fusion | flops 263716864 | bytes 1613824 | tf_op jit(solution)/shard_map/dot_general | solution.py:33
  109.1 1.5 reshape.338
  110.8 0.4 select_reduce_fusion
  111.3 0.2 copy.257
  111.5 0.9 reshape.367
  112.4 4.8 %all-to-all-start.1 = ((f32[128,1,160]{2,1,0:T(1,128)}), f32[128,1,160]{2,1,0:T(1,128)S(1)}, u32[]{:S(2)}, u32[]{:S(2)}) async-start(f32[128,1,160]{2,1,0:T(1,128)} %reshape.367), calls=%async_computation.1 | async-start | bytes 262144 | tf_op jit(solution)/shard_map/all_to_all | solution.py:150
  117.3 9.2 %all-to-all-done.1 = f32[128,1,160]{2,1,0:T(1,128)S(1)} async-done(((f32[128,1,160]{2,1,0:T(1,128)}), f32[128,1,160]{2,1,0:T(1,128)S(1)}, u32[]{:S(2)}, u32[]{:S(2)}) %all-to-all-start.1) | async-done | bytes 81952 | tf_op jit(solution)/shard_map/all_to_all | solution.py:150
  126.5 0.5 broadcast.183
  127.0 1.0 reduce.6
  128.1 0.8 copy.183
  129.0 2.8 %gather_fusion = f32[1024,5]{1,0:T(8,128)S(1)} fusion(f32[5,4096]{0,1:T(8,128)S(1)} %bitcast.127, s32[1024]{0:T(1024)S(1)} %broadcast_clamp_fusion), kind=kCustom, calls=%fused_computation | custom fusion | bytes 45056 | tf_op jit(solution)/shard_map/jit(_take)/gather | solution.py:151
  133.0 1.2 broadcast_in_dim.201
  134.2 4.0 %all-to-all-start.2 = ((f32[32,2,5,8,128]{4,3,2,1,0:T(8,128)}), f32[32,2,5,8,128]{4,3,2,1,0:T(8,128)S(1)}, u32[]{:S(2)}, u32[]{:S(2)}) async-start(f32[32,2,5,8,128]{4,3,2,1,0:T(8,128)} %broadcast_in_dim.201), calls=%async_computation.2 | async-start | bytes 2621440 | tf_op jit(solution)/shard_map/all_to_all | solution.py:180
  138.1 20.6 %all-to-all-done.2 = f32[32,2,5,8,128]{4,3,2,1,0:T(8,128)S(1)} async-done(((f32[32,2,5,8,128]{4,3,2,1,0:T(8,128)}), f32[32,2,5,8,128]{4,3,2,1,0:T(8,128)S(1)}, u32[]{:S(2)}, u32[]{:S(2)}) %all-to-all-start.2) | async-done | bytes 1310752 | tf_op jit(solution)/shard_map/all_to_all | solution.py:180
  158.7 5.0 %shard_map.100 = f32[2,5,8,128]{3,2,1,0:T(8,128)S(1)} custom-call(s32[1]{0:T(128)} %bitcast.24.index_ref, f32[32,75,8,128]{3,2,1,0:T(8,128)} %bitcast.126, f32[32,10,8,128]{3,2,1,0:T(8,128)S(1)} %bitcast.125), custom_call_target="tpu_custom_call" | custom-call | tf_op jit(solution)/shard_map/pallas_call | solution.py:87
  164.3 0.7 copy.190
  (131 shorter events, 7.3 us)
Async XLA Ops:
  6.5 152.2 %all-gather.3.cloned.1.call-start = ((), (), s32[]{:S(2)}) async-start(), calls=%async_computation.3 | async-start | bytes 10137600 | tf_op jit(solution)/shard_map/all_gather | solution.py:132
  10.6 1.4 copy-start.1
  11.1 2.0 %copy-start.7 = (s32[2]{0:T(128)S(1)}, s32[2]{0:T(128)}, u32[]{:S(2)}) copy-start(s32[2]{0:T(128)} %constant.51) | copy-start | bytes 28
  11.9 1.5 copy-start.6
  12.3 2.0 %copy-start.3 = (s32[8,1024]{1,0:T(8,128)S(1)}, s32[8,1024]{1,0:T(8,128)}, u32[]{:S(2)}) copy-start(s32[8,1024]{1,0:T(8,128)} %param.17) | copy-start | bytes 98308
  12.3 2.0 %copy-start.5 = (s32[1024]{0:T(1024)S(1)}, s32[1024]{0:T(1024)}, u32[]{:S(2)}) copy-start(s32[1024]{0:T(1024)} %param.16) | copy-start | bytes 12292
  12.3 2.0 %copy-start.4 = (f32[8,1024]{1,0:T(8,128)S(1)}, f32[8,1024]{1,0:T(8,128)}, u32[]{:S(2)}) copy-start(f32[8,1024]{1,0:T(8,128)} %param.18) | copy-start | bytes 98308
  13.8 77.4 %copy-start.8 = (s32[1,16]{1,0:T(1,128)S(1)}, s32[1,16]{1,0:T(1,128)}, u32[]{:S(2)}) copy-start(s32[1,16]{1,0:T(1,128)} %param.19) | copy-start | bytes 196
  13.8 77.8 %copy-start = (f32[5,2,1024]{2,1,0:T(2,128)S(1)}, f32[5,2,1024]{2,1,0:T(2,128)}, u32[]{:S(2)}) copy-start(f32[5,2,1024]{2,1,0:T(2,128)} %param.10) | copy-start | bytes 122884
  80.0 22.5 %all-to-all-start = ((f32[128,1,544]{2,1,0:T(1,128)}), f32[128,1,544]{2,1,0:T(1,128)S(1)}, u32[]{:S(2)}, u32[]{:S(2)}) async-start(f32[128,1,544]{2,1,0:T(1,128)} %copy.162), calls=%async_computation | async-start | bytes 655360 | tf_op jit(solution)/shard_map/all_to_all | solution.py:146
  112.4 14.1 %all-to-all-start.1 = ((f32[128,1,160]{2,1,0:T(1,128)}), f32[128,1,160]{2,1,0:T(1,128)S(1)}, u32[]{:S(2)}, u32[]{:S(2)}) async-start(f32[128,1,160]{2,1,0:T(1,128)} %reshape.367), calls=%async_computation.1 | async-start | bytes 262144 | tf_op jit(solution)/shard_map/all_to_all | solution.py:150
  128.1 4.3 %copy-start.2 = (f32[5,2,1024]{2,1,0:T(2,128)S(1)}, f32[5,2,1024]{2,1,0:T(2,128)}, u32[]{:S(2)}) copy-start(f32[5,2,1024]{2,1,0:T(2,128)} %param.11) | copy-start | bytes 122884
  134.2 24.5 %all-to-all-start.2 = ((f32[32,2,5,8,128]{4,3,2,1,0:T(8,128)}), f32[32,2,5,8,128]{4,3,2,1,0:T(8,128)S(1)}, u32[]{:S(2)}, u32[]{:S(2)}) async-start(f32[32,2,5,8,128]{4,3,2,1,0:T(8,128)} %broadcast_in_dim.201), calls=%async_computation.2 | async-start | bytes 2621440 | tf_op jit(solution)/shard_map/all_to_all | solution.py:180
Sparse Core Ops, SparseCore 0:
  12.1 58.6 all-gather.2

commit v3 on v1

--- a/solution.py
+++ b/solution.py
@@ -5,8 +5,8 @@
 from jax.experimental.pallas import tpu as pltpu
 from jax.sharding import PartitionSpec as P
 
+
 BLOCK_CELLS = 128
-HIGHEST = lax.Precision.HIGHEST
 
 
 def apply_block(matrix, vector):
@@ -20,17 +20,18 @@
 def interpolate_at_owner(state_flat, request):
     width, resident = state_flat.shape
     blocks = resident // BLOCK_CELLS
-    corners = (request.shape[0] - 1) // 2
-    block = request[0]
-    offs = request[1 : 1 + corners]
-    wts = request[1 + corners :]
+    corners = request.shape[0] // 2
+    wanted = request[:corners]
+    wts = request[corners:]
+    block = jnp.floor(wanted[0] * (1.0 / BLOCK_CELLS))
     lanes = lax.broadcasted_iota(jnp.float32, (BLOCK_CELLS, 1), 0)
     spread = jnp.zeros((BLOCK_CELLS, request.shape[1]), jnp.float32)
     for k in range(corners):
-        spread = spread + jnp.where(offs[k][None, :] == lanes, wts[k][None, :], 0.0)
+        offs = wanted[k] - block * BLOCK_CELLS
+        spread = spread + jnp.where(offs[None, :] == lanes, wts[k][None, :], 0.0)
     table = state_flat.reshape(width, blocks, BLOCK_CELLS).transpose(1, 0, 2)
     table = table.reshape(blocks * width, BLOCK_CELLS)
-    every = jnp.dot(table, spread, precision=HIGHEST).reshape(blocks, width, -1)
+    every = jnp.dot(table, spread, precision=lax.Precision.HIGH).reshape(blocks, width, -1)
     ids = lax.broadcasted_iota(jnp.float32, (blocks, 1, 1), 0)
     return jnp.sum(jnp.where(block[None, None, :] == ids, every, 0.0), axis=0)
 
@@ -98,7 +99,7 @@
     )(index, all_maps, every)
 
 
-def body(
+def sweep_body(
     state, rhs, dinv, lower_jac, upper_jac, owner, donor_block, offsets, weights, receptor_perm
 ):
     width, planes, cells = state.shape
@@ -136,9 +137,8 @@
     onehot = (target[:, None] == jnp.arange(devices, dtype=jnp.int32)[None, :]).astype(jnp.int32)
     slot = jnp.sum(jnp.cumsum(onehot, axis=0) * onehot, axis=1) - 1
     flat_slot = target * capacity + slot
-    payload = jnp.concatenate(
-        [donor_block[None, :].astype(jnp.float32), offsets.astype(jnp.float32), weights], axis=0
-    )
+    cells_wanted = donor_block[None, :] * BLOCK_CELLS + offsets
+    payload = jnp.concatenate([cells_wanted.astype(jnp.float32), weights], axis=0)
     request = jnp.zeros((payload.shape[0], devices * capacity), jnp.float32)
     request = request.at[:, flat_slot].set(payload).reshape(-1, devices, capacity)
     received = lax.all_to_all(request, ("slab", "cross"), split_axis=1, concat_axis=1, tiled=True)
@@ -201,7 +201,7 @@
 
 def solution(mesh):
     return jax.shard_map(
-        body,
+        sweep_body,
         mesh=mesh,
         in_specs=(
             P(None, "slab", "cross"),

time: 118 us -> 114 us (0.966)
  waiting for transfers between devices: 40.3 us -> 37.6 us
  local copies, waits for them, and re-layouts: 27 us -> 25.2 us
  other arithmetic: 6.5 us -> 7.85 us
    all_to_all x3, waiting for transfers between devices: 40.3 us -> 37.6 us  [the longest x1 20.6 us: sweep_body(): every = lax.all_to_all(spread, 'slab', 0, 0, tiled=True)]
    unnamed x23 -> x35, local copies, waits for them, and re-layouts: 4.27 us -> 2.63 us
    reshape x6, local copies, waits for them, and re-layouts: 3.87 us -> 2.51 us  [the longest x1 1.52 us: interpolate_at_owner(): jnp.dot(table, spread, precision=lax.Precision.HIGH)]
  transfers between devices with their start and end apart: 4 -> 4, of which waited for: 3 -> 3; matrix products, arithmetic and copies ran while one was open for 27% -> 26% of each run, Pallas kernels for 0% -> 0%
where the time goes in v3:
time: 114 us; the launch traced here: 113 us
  waiting for transfers between devices  37.6 us (33%)
  local copies, waits for them, and re-layouts  25.2 us (22%)
  starting transfers between devices  20 us (18%)
  between operations  14.1 us (12%)
  other arithmetic  7.85 us (7%)
  Pallas kernels  4.99 us (4%)
  matrix products  3.41 us (3%)
    all_to_all x1, waiting for transfers between devices, sweep_body(): every = lax.all_to_all(spread, 'slab', 0, 0, tiled=True)  20.6 us
    all_to_all x1, starting transfers between devices, sweep_body(): lax.all_to_all(request, ('slab', 'cross'), split_axis=1, concat_axis=1, t...  11.4 us
    all_to_all x1, waiting for transfers between devices, sweep_body(): lax.all_to_all(answer, ('slab', 'cross'), split_axis=1, concat_axis=1, ti...  9.39 us
    all_to_all x1, waiting for transfers between devices, sweep_body(): lax.all_to_all(request, ('slab', 'cross'), split_axis=1, concat_axis=1, t...  7.62 us
    pallas_call x1, Pallas kernels, fold_entries(): pl.pallas_call(fold_kernel, out_shape=jax.ShapeDtypeStruct((2, width, sub...  4.99 us
    all_to_all x1, starting transfers between devices, sweep_body(): lax.all_to_all(answer, ('slab', 'cross'), split_axis=1, concat_axis=1, ti...  4.68 us
    all_to_all x1, starting transfers between devices, sweep_body(): every = lax.all_to_all(spread, 'slab', 0, 0, tiled=True)  3.95 us
    scatter x1, local copies, waits for them, and re-layouts, sweep_body(): request.at[:, flat_slot].set(payload).reshape(-1, devices, capacity)  3.59 us
  transfers between devices with their start and end apart: 4, of which 3 were waited for; matrix products, arithmetic and copies ran while one was open for 26% of the time, Pallas kernels for 0%

profile of v3, /device:TPU:0, one launch (start us, length us, event | category | flops | bytes accessed | tf_op | source)
XLA Modules:
  0.0 113.1 jit_solution(9449642899011379232)
XLA Ops:
  6.5 1.2 %fusion.40 = (f32[5,5,1,1024]{3,2,1,0:T(1,128)S(1)}, f32[5,5,1,1024]{3,2,1,0:T(1,128)S(1)}) fusion(f32[5,5,2,1024]{3,2,1,0:T(2,128)} %param.13), kind=kLoop, calls=%fused_computation.142 | loop fusion | bytes 409600 | tf_op jit(solution)/shard_map/slice | solution.py:118
  7.8 1.3 %fusion.42 = (f32[5,5,1,1024]{3,2,1,0:T(1,128)S(1)}, f32[5,5,1,1024]{3,2,1,0:T(1,128)S(1)}) fusion(f32[5,5,2,1024]{3,2,1,0:T(2,128)} %param.12), kind=kLoop, calls=%fused_computation.144 | loop fusion | bytes 409600 | tf_op jit(solution)/shard_map/slice | solution.py:189
  9.1 1.2 %fusion.41 = (f32[5,5,1,1024]{3,2,1,0:T(1,128)S(1)}, f32[5,5,1,1024]{3,2,1,0:T(1,128)S(1)}) fusion(f32[5,5,2,1024]{3,2,1,0:T(2,128)} %param.14), kind=kLoop, calls=%fused_computation.143 | loop fusion | bytes 409600 | tf_op jit(solution)/shard_map/slice | solution.py:122
  11.3 0.8 pad_maximum_fusion
  12.9 0.4 fusion.34
  13.2 0.6 and_reduce_fusion
  13.9 3.6 %scatter_custom_fusion = f32[16,4096]{0,1:T(8,128)S(1)} fusion(s32[1024]{0:T(1024)S(1)} %bitcast.134, f32[1024,16]{1,0:T(8,128)S(1)} %copy.77, f32[]{:T(128)} %constant.19.clone.1), kind=kCustom, calls=%fused_computation.44 | custom fusion | bytes 262148 | tf_op jit(solution)/shard_map/scatter | solution.py:143
  17.5 0.6 copy.78
  18.1 1.2 %reshape.453 = f32[128,1,512]{2,1,0:T(1,128)} reshape(f32[128,16,32]{2,1,0:T(8,128)S(1)} %bitcast.121) | data formatting | bytes 524288
  19.2 11.4 %all-to-all-start = ((f32[128,1,512]{2,1,0:T(1,128)}), f32[128,1,512]{2,1,0:T(1,128)S(1)}, u32[]{:S(2)}, u32[]{:S(2)}) async-start(f32[128,1,512]{2,1,0:T(1,128)} %reshape.453), calls=%async_computation | async-start | bytes 524288 | tf_op jit(solution)/shard_map/all_to_all | solution.py:144
  30.6 0.7 slice_bitcast_fusion.3
  31.5 1.0 multiply_reduce_fusion.22
  32.5 0.8 reshape_reshape.4
  33.5 7.6 %all-to-all-done = f32[128,1,512]{2,1,0:T(1,128)S(1)} async-done(((f32[128,1,512]{2,1,0:T(1,128)}), f32[128,1,512]{2,1,0:T(1,128)S(1)}, u32[]{:S(2)}, u32[]{:S(2)}) %all-to-all-start) | async-done | bytes 262176 | tf_op jit(solution)/shard_map/all_to_all | solution.py:144
  41.1 0.5 broadcast.220
  41.6 1.3 %reduce.66 = f32[128,512]{1,0:T(8,128)S(1)} reduce(f32[128,1,512]{2,1,0:T(1,128)S(1)} %all-to-all-done, f32[]{:T(128)} %broadcast.220), dimensions={1}, to_apply=%all_to_all.9.reduce_sub_computation | reduce | bytes 524292 | tf_op jit(solution)/shard_map/all_to_all | solution.py:144
  42.9 0.3 reshape.454
  43.1 3.0 %slice_reduce_fusion.14 = (f32[128,32]{1,0:T(8,128)S(1)}, f32[128,32]{1,0:T(8,128)S(1)}, f32[128,32]{1,0:T(8,128)S(1)}, f32[128,32]{1,0:T(8,128)S(1)}, f32[128,3...) fusion(f32[16,128,32]{2,0,1:T(8,128)S(1)} %bitcast.122), kind=kLoop, calls=%fused_computation.101 | loop fusion | bytes 524288 | tf_op jit(solution)/shard_map/slice | solution.py:31
  47.5 3.4 %convolution_bitcast_fusion = f32[80,4096]{1,0:T(8,128)} fusion(f32[80,128]{1,0:T(8,128)S(1)} %reshape.343, f32[4096]{0:T(1024)S(1)} %broadcast_in_dim.195, f32[4096]{0:T(1024)S(1)} %get-tuple-element.44, f32[4096]{0:T(1024)S(1)} %broadcast_in_dim.193, f32[4096]{0:T(1024)S(1)} %get-tuple-element.45, f32[4096]{0:T(1024)S(1)} %broadcast_in_dim.191, ...), kind=kOutput, calls=%fused_computation.2 | convolution fusion | flops 263716864 | bytes 1613824 | tf_op jit(solution)/shard_map/dot_general | solution.py:34
  50.9 1.5 %reshape.344 = f32[16,5,4096]{2,1,0:T(8,128)S(1)} reshape(f32[80,4096]{1,0:T(8,128)} %convolution_bitcast_fusion) | data formatting | bytes 2621440 | tf_op jit(solution)/shard_map/reshape | solution.py:34
  52.4 0.4 select_reduce_fusion
  53.2 0.9 reshape.455
  54.1 4.7 %all-to-all-start.1 = ((f32[128,1,160]{2,1,0:T(1,128)}), f32[128,1,160]{2,1,0:T(1,128)S(1)}, u32[]{:S(2)}, u32[]{:S(2)}) async-start(f32[128,1,160]{2,1,0:T(1,128)} %reshape.455), calls=%async_computation.1 | async-start | bytes 262144 | tf_op jit(solution)/shard_map/all_to_all | solution.py:147
  58.8 9.4 %all-to-all-done.1 = f32[128,1,160]{2,1,0:T(1,128)S(1)} async-done(((f32[128,1,160]{2,1,0:T(1,128)}), f32[128,1,160]{2,1,0:T(1,128)S(1)}, u32[]{:S(2)}, u32[]{:S(2)}) %all-to-all-start.1) | async-done | bytes 81952 | tf_op jit(solution)/shard_map/all_to_all | solution.py:147
  68.2 1.0 reduce.67
  69.3 0.8 copy.81
  70.2 2.8 %gather_fusion = f32[1024,5]{1,0:T(8,128)S(1)} fusion(f32[5,4096]{0,1:T(8,128)S(1)} %bitcast.123, s32[1024]{0:T(1024)S(1)} %broadcast_clamp_fusion), kind=kCustom, calls=%fused_computation | custom fusion | bytes 45056 | tf_op jit(solution)/shard_map/jit(_take)/gather | solution.py:148
  74.3 1.2 %broadcast_in_dim.202 = f32[32,2,5,8,128]{4,3,2,1,0:T(8,128)} broadcast(f32[2,5,8,128]{3,2,1,0:T(8,128)S(1)} %maximum_bitcast_fusion.1), dimensions={1,2,3,4} | broadcast | bytes 1351680 | tf_op jit(solution)/shard_map/broadcast_in_dim | solution.py:176
  75.4 4.0 %all-to-all-start.2 = ((f32[32,2,5,8,128]{4,3,2,1,0:T(8,128)}), f32[32,2,5,8,128]{4,3,2,1,0:T(8,128)S(1)}, u32[]{:S(2)}, u32[]{:S(2)}) async-start(f32[32,2,5,8,128]{4,3,2,1,0:T(8,128)} %broadcast_in_dim.202), calls=%async_computation.2 | async-start | bytes 2621440 | tf_op jit(solution)/shard_map/all_to_all | solution.py:177
  79.4 20.6 %all-to-all-done.2 = f32[32,2,5,8,128]{4,3,2,1,0:T(8,128)S(1)} async-done(((f32[32,2,5,8,128]{4,3,2,1,0:T(8,128)}), f32[32,2,5,8,128]{4,3,2,1,0:T(8,128)S(1)}, u32[]{:S(2)}, u32[]{:S(2)}) %all-to-all-start.2) | async-done | bytes 1310752 | tf_op jit(solution)/shard_map/all_to_all | solution.py:177
  99.9 5.0 %shard_map.100 = f32[2,5,8,128]{3,2,1,0:T(8,128)S(1)} custom-call(s32[1]{0:T(128)} %bitcast.17.index_ref, f32[32,75,8,128]{3,2,1,0:T(8,128)} %bitcast.119, f32[32,10,8,128]{3,2,1,0:T(8,128)S(1)} %bitcast.118), custom_call_target="tpu_custom_call" | custom-call | tf_op jit(solution)/shard_map/pallas_call | solution.py:88
  105.6 0.7 copy.88
  (114 shorter events, 5.6 us)
Async XLA Ops:
  6.5 93.4 %all-gather.3.cloned.1.call-start = ((), (), s32[]{:S(2)}) async-start(), calls=%async_computation.3 | async-start | bytes 10137600 | tf_op jit(solution)/shard_map/all_gather | solution.py:133
  7.7 2.7 %copy-start = (f32[5,5,1,1024]{3,2,1,0:T(1,128)}, f32[5,5,1,1024]{3,2,1,0:T(1,128)S(1)}, u32[]{:S(2)}) copy-start(f32[5,5,1,1024]{3,2,1,0:T(1,128)S(1)} %get-tuple-element.33) | copy-start | bytes 307204
  7.8 2.7 %copy-start.2 = (f32[5,5,1,1024]{3,2,1,0:T(1,128)}, f32[5,5,1,1024]{3,2,1,0:T(1,128)S(1)}, u32[]{:S(2)}) copy-start(f32[5,5,1,1024]{3,2,1,0:T(1,128)S(1)} %get-tuple-element.34) | copy-start | bytes 307204
  10.7 1.4 %copy-start.6 = (s32[1024,1]{0,1:T(1,128)S(1)}, s32[1024,1]{0,1:T(1,128)}, u32[]{:S(2)}) copy-start(s32[1024,1]{0,1:T(1,128)} %param.15) | copy-start | bytes 12292
  11.2 1.4 %copy-start.12 = (s32[1024]{0:T(1024)S(1)}, s32[1024]{0:T(1024)}, u32[]{:S(2)}) copy-start(s32[1024]{0:T(1024)} %param.16) | copy-start | bytes 12292
  11.2 1.4 %copy-start.7 = (s32[8,1024]{1,0:T(8,128)S(1)}, s32[8,1024]{1,0:T(8,128)}, u32[]{:S(2)}) copy-start(s32[8,1024]{1,0:T(8,128)} %param.17) | copy-start | bytes 98308
  11.2 1.4 %copy-start.8 = (f32[8,1024]{1,0:T(8,128)S(1)}, f32[8,1024]{1,0:T(8,128)}, u32[]{:S(2)}) copy-start(f32[8,1024]{1,0:T(8,128)} %param.18) | copy-start | bytes 98308
  13.9 3.6 %copy-start.9 = (s32[1024,1]{0,1:T(1,128)}, s32[1024,1]{0,1:T(1,128)S(1)}, u32[]{:S(2)}) copy-start(s32[1024,1]{0,1:T(1,128)S(1)} %get-tuple-element.32) | copy-start | bytes 12292
  18.1 15.4 %copy-start.10 = (s32[1024,1]{0,1:T(1,128)S(1)}, s32[1024,1]{0,1:T(1,128)}, u32[]{:S(2)}) copy-start(s32[1024,1]{0,1:T(1,128)} %copy-done.9) | copy-start | bytes 12292
  19.2 21.8 %all-to-all-start = ((f32[128,1,512]{2,1,0:T(1,128)}), f32[128,1,512]{2,1,0:T(1,128)S(1)}, u32[]{:S(2)}, u32[]{:S(2)}) async-start(f32[128,1,512]{2,1,0:T(1,128)} %reshape.453), calls=%async_computation | async-start | bytes 524288 | tf_op jit(solution)/shard_map/all_to_all | solution.py:144
  54.1 18.9 %copy-start.11 = (pred[1024]{0:T(1024)(128)(4,1)S(1)}, pred[1024]{0:T(1024)(128)(4,1)}, u32[]{:S(2)}) copy-start(pred[1024]{0:T(1024)(128)(4,1)} %get-tuple-element.31) | copy-start | bytes 3076
  54.1 14.2 %all-to-all-start.1 = ((f32[128,1,160]{2,1,0:T(1,128)}), f32[128,1,160]{2,1,0:T(1,128)S(1)}, u32[]{:S(2)}, u32[]{:S(2)}) async-start(f32[128,1,160]{2,1,0:T(1,128)} %reshape.455), calls=%async_computation.1 | async-start | bytes 262144 | tf_op jit(solution)/shard_map/all_to_all | solution.py:147
  69.3 4.3 %copy-start.4 = (f32[5,2,1024]{2,1,0:T(2,128)S(1)}, f32[5,2,1024]{2,1,0:T(2,128)}, u32[]{:S(2)}) copy-start(f32[5,2,1024]{2,1,0:T(2,128)} %param.10) | copy-start | bytes 122884
  69.3 4.3 %copy-start.5 = (f32[5,2,1024]{2,1,0:T(2,128)S(1)}, f32[5,2,1024]{2,1,0:T(2,128)}, u32[]{:S(2)}) copy-start(f32[5,2,1024]{2,1,0:T(2,128)} %param.11) | copy-start | bytes 122884
  69.3 4.5 %copy-start.1 = (f32[5,5,1,1024]{3,2,1,0:T(1,128)S(1)}, f32[5,5,1,1024]{3,2,1,0:T(1,128)}, u32[]{:S(2)}) copy-start(f32[5,5,1,1024]{3,2,1,0:T(1,128)} %copy-done) | copy-start | bytes 307204
  75.4 24.5 %all-to-all-start.2 = ((f32[32,2,5,8,128]{4,3,2,1,0:T(8,128)}), f32[32,2,5,8,128]{4,3,2,1,0:T(8,128)S(1)}, u32[]{:S(2)}, u32[]{:S(2)}) async-start(f32[32,2,5,8,128]{4,3,2,1,0:T(8,128)} %broadcast_in_dim.202), calls=%async_computation.2 | async-start | bytes 2621440 | tf_op jit(solution)/shard_map/all_to_all | solution.py:177
  99.9 5.0 %copy-start.3 = (f32[5,5,1,1024]{3,2,1,0:T(1,128)S(1)}, f32[5,5,1,1024]{3,2,1,0:T(1,128)}, u32[]{:S(2)}) copy-start(f32[5,5,1,1024]{3,2,1,0:T(1,128)} %copy-done.2) | copy-start | bytes 307204
Sparse Core Ops, SparseCore 0:
  12.2 62.6 all-gather.2

commit v4 on v3

--- a/solution.py
+++ b/solution.py
@@ -4,7 +4,6 @@
 from jax.experimental import pallas as pl
 from jax.experimental.pallas import tpu as pltpu
 from jax.sharding import PartitionSpec as P
-
 
 BLOCK_CELLS = 128
 
@@ -29,11 +28,12 @@
     for k in range(corners):
         offs = wanted[k] - block * BLOCK_CELLS
         spread = spread + jnp.where(offs[None, :] == lanes, wts[k][None, :], 0.0)
+    rows = 8
     table = state_flat.reshape(width, blocks, BLOCK_CELLS).transpose(1, 0, 2)
-    table = table.reshape(blocks * width, BLOCK_CELLS)
-    every = jnp.dot(table, spread, precision=lax.Precision.HIGH).reshape(blocks, width, -1)
+    table = jnp.pad(table, ((0, 0), (0, rows - width), (0, 0))).reshape(blocks * rows, BLOCK_CELLS)
+    every = jnp.dot(table, spread, precision=lax.Precision.HIGH).reshape(blocks, rows, -1)
     ids = lax.broadcasted_iota(jnp.float32, (blocks, 1, 1), 0)
-    return jnp.sum(jnp.where(block[None, None, :] == ids, every, 0.0), axis=0)
+    return jnp.sum(jnp.where(block[None, None, :] == ids, every, 0.0), axis=0)[:width]
 
 
 def fold_kernel(index_ref, maps_ref, offsets_ref, out_ref, up_ref):

time: 114 us -> 111 us (0.974)
  local copies, waits for them, and re-layouts: 25.2 us -> 23.7 us
    reshape x2 -> x0, local copies, waits for them, and re-layouts: 1.53 us -> none  [the longest x1 1.52 us: interpolate_at_owner(): jnp.dot(table, spread, precision=lax.Precision.HIGH)]
  transfers between devices with their start and end apart: 4 -> 4, of which waited for: 3 -> 3; matrix products, arithmetic and copies ran while one was open for 26% -> 25% of each run, Pallas kernels for 0% -> 0%
where the time goes in v4:
time: 111 us
  waiting for transfers between devices  37.6 us (34%)
  local copies, waits for them, and re-layouts  23.7 us (21%)
  starting transfers between devices  20 us (18%)
  between operations  14.1 us (13%)
  other arithmetic  7.48 us (7%)
  Pallas kernels  4.99 us (4%)
  matrix products  2.89 us (3%)
    all_to_all x1, waiting for transfers between devices, sweep_body(): every = lax.all_to_all(spread, 'slab', 0, 0, tiled=True)  20.6 us
    all_to_all x1, starting transfers between devices, sweep_body(): lax.all_to_all(request, ('slab', 'cross'), split_axis=1, concat_axis=1, t...  11.4 us
    all_to_all x1, waiting for transfers between devices, sweep_body(): lax.all_to_all(answer, ('slab', 'cross'), split_axis=1, concat_axis=1, ti...  9.39 us
    all_to_all x1, waiting for transfers between devices, sweep_body(): lax.all_to_all(request, ('slab', 'cross'), split_axis=1, concat_axis=1, t...  7.63 us
    pallas_call x1, Pallas kernels, fold_entries(): pl.pallas_call(fold_kernel, out_shape=jax.ShapeDtypeStruct((2, width, sub...  4.99 us
    all_to_all x1, starting transfers between devices, sweep_body(): lax.all_to_all(answer, ('slab', 'cross'), split_axis=1, concat_axis=1, ti...  4.68 us
    all_to_all x1, starting transfers between devices, sweep_body(): every = lax.all_to_all(spread, 'slab', 0, 0, tiled=True)  3.95 us
    scatter x1, local copies, waits for them, and re-layouts, sweep_body(): request.at[:, flat_slot].set(payload).reshape(-1, devices, capacity)  3.59 us
  transfers between devices with their start and end apart: 4, of which 3 were waited for; matrix products, arithmetic and copies ran while one was open for 25% of the time, Pallas kernels for 0%

profile of v4, /device:TPU:0, one launch (start us, length us, event | category | flops | bytes accessed | tf_op | source)
XLA Modules:
  0.0 110.7 jit_solution(8016866449897531521)
XLA Ops:
  6.5 1.2 %fusion.45 = (f32[5,5,1,1024]{3,2,1,0:T(1,128)S(1)}, f32[5,5,1,1024]{3,2,1,0:T(1,128)S(1)}) fusion(f32[5,5,2,1024]{3,2,1,0:T(2,128)} %param.13), kind=kLoop, calls=%fused_computation.144 | loop fusion | bytes 409600 | tf_op jit(solution)/shard_map/slice | solution.py:118
  7.8 1.3 %fusion.47 = (f32[5,5,1,1024]{3,2,1,0:T(1,128)S(1)}, f32[5,5,1,1024]{3,2,1,0:T(1,128)S(1)}) fusion(f32[5,5,2,1024]{3,2,1,0:T(2,128)} %param.12), kind=kLoop, calls=%fused_computation.146 | loop fusion | bytes 409600 | tf_op jit(solution)/shard_map/slice | solution.py:189
  9.1 1.2 %fusion.46 = (f32[5,5,1,1024]{3,2,1,0:T(1,128)S(1)}, f32[5,5,1,1024]{3,2,1,0:T(1,128)S(1)}) fusion(f32[5,5,2,1024]{3,2,1,0:T(2,128)} %param.14), kind=kLoop, calls=%fused_computation.145 | loop fusion | bytes 409600 | tf_op jit(solution)/shard_map/slice | solution.py:122
  11.3 0.8 pad_maximum_fusion
  12.2 0.2 fusion.39
  12.9 0.4 fusion.38
  13.2 0.6 and_reduce_fusion
  13.9 3.6 %scatter_custom_fusion = f32[16,4096]{0,1:T(8,128)S(1)} fusion(s32[1024]{0:T(1024)S(1)} %bitcast.138, f32[1024,16]{1,0:T(8,128)S(1)} %copy.77, f32[]{:T(128)} %constant.20.clone.1), kind=kCustom, calls=%fused_computation.45 | custom fusion | bytes 262148 | tf_op jit(solution)/shard_map/scatter | solution.py:143
  17.5 0.6 copy.78
  18.1 1.2 %reshape.450 = f32[128,1,512]{2,1,0:T(1,128)} reshape(f32[128,16,32]{2,1,0:T(8,128)S(1)} %bitcast.124) | data formatting | bytes 524288
  19.2 11.4 %all-to-all-start = ((f32[128,1,512]{2,1,0:T(1,128)}), f32[128,1,512]{2,1,0:T(1,128)S(1)}, u32[]{:S(2)}, u32[]{:S(2)}) async-start(f32[128,1,512]{2,1,0:T(1,128)} %reshape.450), calls=%async_computation | async-start | bytes 524288 | tf_op jit(solution)/shard_map/all_to_all | solution.py:144
  30.6 0.7 slice_bitcast_fusion.3
  31.5 1.0 multiply_reduce_fusion.22
  32.5 0.8 reshape_reshape.4
  33.4 7.6 %all-to-all-done = f32[128,1,512]{2,1,0:T(1,128)S(1)} async-done(((f32[128,1,512]{2,1,0:T(1,128)}), f32[128,1,512]{2,1,0:T(1,128)S(1)}, u32[]{:S(2)}, u32[]{:S(2)}) %all-to-all-start) | async-done | bytes 262176 | tf_op jit(solution)/shard_map/all_to_all | solution.py:144
  41.1 0.5 broadcast.222
  41.6 1.3 %reduce.66 = f32[128,512]{1,0:T(8,128)S(1)} reduce(f32[128,1,512]{2,1,0:T(1,128)S(1)} %all-to-all-done, f32[]{:T(128)} %broadcast.222), dimensions={1}, to_apply=%all_to_all.9.reduce_sub_computation | reduce | bytes 524292 | tf_op jit(solution)/shard_map/all_to_all | solution.py:144
  42.9 0.3 reshape.451
  43.1 3.0 %slice_reduce_fusion.14 = (f32[128,32]{1,0:T(8,128)S(1)}, f32[128,32]{1,0:T(8,128)S(1)}, f32[128,32]{1,0:T(8,128)S(1)}, f32[128,32]{1,0:T(8,128)S(1)}, f32[128,3...) fusion(f32[16,128,32]{2,0,1:T(8,128)S(1)} %bitcast.125), kind=kLoop, calls=%fused_computation.102 | loop fusion | bytes 524288 | tf_op jit(solution)/shard_map/slice | solution.py:30
  47.5 2.9 %fusion.16 = f32[8,4096]{1,0:T(8,128)S(1)} fusion(f32[4096]{0:T(1024)S(1)} %broadcast_in_dim.195, f32[4096]{0:T(1024)S(1)} %get-tuple-element.44, f32[4096]{0:T(1024)S(1)} %broadcast_in_dim.193, f32[4096]{0:T(1024)S(1)} %get-tuple-element.45, f32[4096]{0:T(1024)S(1)} %broadcast_in_dim.191, f32[4096]{0:T(1024)S(1)} %get-tuple-element.46, ...), kind=kOutput, calls=%fused_computation.27 | convolution fusion | flops 415727616 | bytes 499712 | tf_op jit(solution)/shard_map/dot_general | solution.py:34
  50.5 0.2 copy.155
  50.7 0.9 reshape.452
  51.6 4.7 %all-to-all-start.1 = ((f32[128,1,160]{2,1,0:T(1,128)}), f32[128,1,160]{2,1,0:T(1,128)S(1)}, u32[]{:S(2)}, u32[]{:S(2)}) async-start(f32[128,1,160]{2,1,0:T(1,128)} %reshape.452), calls=%async_computation.1 | async-start | bytes 262144 | tf_op jit(solution)/shard_map/all_to_all | solution.py:147
  56.4 9.4 %all-to-all-done.1 = f32[128,1,160]{2,1,0:T(1,128)S(1)} async-done(((f32[128,1,160]{2,1,0:T(1,128)}), f32[128,1,160]{2,1,0:T(1,128)S(1)}, u32[]{:S(2)}, u32[]{:S(2)}) %all-to-all-start.1) | async-done | bytes 81952 | tf_op jit(solution)/shard_map/all_to_all | solution.py:147
  65.8 1.0 reduce.67
  66.9 0.8 copy.81
  67.8 2.8 %gather_fusion = f32[1024,5]{1,0:T(8,128)S(1)} fusion(f32[5,4096]{0,1:T(8,128)S(1)} %bitcast.126, s32[1024]{0:T(1024)S(1)} %broadcast_clamp_fusion), kind=kCustom, calls=%fused_computation | custom fusion | bytes 45056 | tf_op jit(solution)/shard_map/jit(_take)/gather | solution.py:148
  71.8 1.2 %broadcast_in_dim.202 = f32[32,2,5,8,128]{4,3,2,1,0:T(8,128)} broadcast(f32[2,5,8,128]{3,2,1,0:T(8,128)S(1)} %maximum_bitcast_fusion.1), dimensions={1,2,3,4} | broadcast | bytes 1351680 | tf_op jit(solution)/shard_map/broadcast_in_dim | solution.py:176
  73.0 4.0 %all-to-all-start.2 = ((f32[32,2,5,8,128]{4,3,2,1,0:T(8,128)}), f32[32,2,5,8,128]{4,3,2,1,0:T(8,128)S(1)}, u32[]{:S(2)}, u32[]{:S(2)}) async-start(f32[32,2,5,8,128]{4,3,2,1,0:T(8,128)} %broadcast_in_dim.202), calls=%async_computation.2 | async-start | bytes 2621440 | tf_op jit(solution)/shard_map/all_to_all | solution.py:177
  77.0 20.6 %all-to-all-done.2 = f32[32,2,5,8,128]{4,3,2,1,0:T(8,128)S(1)} async-done(((f32[32,2,5,8,128]{4,3,2,1,0:T(8,128)}), f32[32,2,5,8,128]{4,3,2,1,0:T(8,128)S(1)}, u32[]{:S(2)}, u32[]{:S(2)}) %all-to-all-start.2) | async-done | bytes 1310752 | tf_op jit(solution)/shard_map/all_to_all | solution.py:177
  97.5 5.0 %shard_map.100 = f32[2,5,8,128]{3,2,1,0:T(8,128)S(1)} custom-call(s32[1]{0:T(128)} %bitcast.17.index_ref, f32[32,75,8,128]{3,2,1,0:T(8,128)} %bitcast.122, f32[32,10,8,128]{3,2,1,0:T(8,128)S(1)} %bitcast.121), custom_call_target="tpu_custom_call" | custom-call | tf_op jit(solution)/shard_map/pallas_call | solution.py:88
  103.2 0.7 copy.88
  (111 shorter events, 5.2 us)
Async XLA Ops:
  6.5 91.0 %all-gather.3.cloned.1.call-start = ((), (), s32[]{:S(2)}) async-start(), calls=%async_computation.3 | async-start | bytes 10137600 | tf_op jit(solution)/shard_map/all_gather | solution.py:133
  7.7 2.7 %copy-start = (f32[5,5,1,1024]{3,2,1,0:T(1,128)}, f32[5,5,1,1024]{3,2,1,0:T(1,128)S(1)}, u32[]{:S(2)}) copy-start(f32[5,5,1,1024]{3,2,1,0:T(1,128)S(1)} %get-tuple-element.33) | copy-start | bytes 307204
  7.8 2.7 %copy-start.2 = (f32[5,5,1,1024]{3,2,1,0:T(1,128)}, f32[5,5,1,1024]{3,2,1,0:T(1,128)S(1)}, u32[]{:S(2)}) copy-start(f32[5,5,1,1024]{3,2,1,0:T(1,128)S(1)} %get-tuple-element.34) | copy-start | bytes 307204
  10.7 1.4 %copy-start.6 = (s32[1024,1]{0,1:T(1,128)S(1)}, s32[1024,1]{0,1:T(1,128)}, u32[]{:S(2)}) copy-start(s32[1024,1]{0,1:T(1,128)} %param.15) | copy-start | bytes 12292
  11.2 1.4 %copy-start.12 = (s32[1024]{0:T(1024)S(1)}, s32[1024]{0:T(1024)}, u32[]{:S(2)}) copy-start(s32[1024]{0:T(1024)} %param.16) | copy-start | bytes 12292
  11.2 1.4 %copy-start.7 = (s32[8,1024]{1,0:T(8,128)S(1)}, s32[8,1024]{1,0:T(8,128)}, u32[]{:S(2)}) copy-start(s32[8,1024]{1,0:T(8,128)} %param.17) | copy-start | bytes 98308
  11.2 1.4 %copy-start.8 = (f32[8,1024]{1,0:T(8,128)S(1)}, f32[8,1024]{1,0:T(8,128)}, u32[]{:S(2)}) copy-start(f32[8,1024]{1,0:T(8,128)} %param.18) | copy-start | bytes 98308
  13.9 3.6 %copy-start.9 = (s32[1024,1]{0,1:T(1,128)}, s32[1024,1]{0,1:T(1,128)S(1)}, u32[]{:S(2)}) copy-start(s32[1024,1]{0,1:T(1,128)S(1)} %get-tuple-element.32) | copy-start | bytes 12292
  18.1 15.3 %copy-start.10 = (s32[1024,1]{0,1:T(1,128)S(1)}, s32[1024,1]{0,1:T(1,128)}, u32[]{:S(2)}) copy-start(s32[1024,1]{0,1:T(1,128)} %copy-done.9) | copy-start | bytes 12292
  19.2 21.8 %all-to-all-start = ((f32[128,1,512]{2,1,0:T(1,128)}), f32[128,1,512]{2,1,0:T(1,128)S(1)}, u32[]{:S(2)}, u32[]{:S(2)}) async-start(f32[128,1,512]{2,1,0:T(1,128)} %reshape.450), calls=%async_computation | async-start | bytes 524288 | tf_op jit(solution)/shard_map/all_to_all | solution.py:144
  51.6 18.9 %copy-start.11 = (pred[1024]{0:T(1024)(128)(4,1)S(1)}, pred[1024]{0:T(1024)(128)(4,1)}, u32[]{:S(2)}) copy-start(pred[1024]{0:T(1024)(128)(4,1)} %get-tuple-element.31) | copy-start | bytes 3076
  51.6 14.2 %all-to-all-start.1 = ((f32[128,1,160]{2,1,0:T(1,128)}), f32[128,1,160]{2,1,0:T(1,128)S(1)}, u32[]{:S(2)}, u32[]{:S(2)}) async-start(f32[128,1,160]{2,1,0:T(1,128)} %reshape.452), calls=%async_computation.1 | async-start | bytes 262144 | tf_op jit(solution)/shard_map/all_to_all | solution.py:147
  66.9 4.3 %copy-start.4 = (f32[5,2,1024]{2,1,0:T(2,128)S(1)}, f32[5,2,1024]{2,1,0:T(2,128)}, u32[]{:S(2)}) copy-start(f32[5,2,1024]{2,1,0:T(2,128)} %param.10) | copy-start | bytes 122884
  66.9 4.3 %copy-start.5 = (f32[5,2,1024]{2,1,0:T(2,128)S(1)}, f32[5,2,1024]{2,1,0:T(2,128)}, u32[]{:S(2)}) copy-start(f32[5,2,1024]{2,1,0:T(2,128)} %param.11) | copy-start | bytes 122884
  66.9 4.5 %copy-start.1 = (f32[5,5,1,1024]{3,2,1,0:T(1,128)S(1)}, f32[5,5,1,1024]{3,2,1,0:T(1,128)}, u32[]{:S(2)}) copy-start(f32[5,5,1,1024]{3,2,1,0:T(1,128)} %copy-done) | copy-start | bytes 307204
  73.0 24.5 %all-to-all-start.2 = ((f32[32,2,5,8,128]{4,3,2,1,0:T(8,128)}), f32[32,2,5,8,128]{4,3,2,1,0:T(8,128)S(1)}, u32[]{:S(2)}, u32[]{:S(2)}) async-start(f32[32,2,5,8,128]{4,3,2,1,0:T(8,128)} %broadcast_in_dim.202), calls=%async_computation.2 | async-start | bytes 2621440 | tf_op jit(solution)/shard_map/all_to_all | solution.py:177
  97.5 5.0 %copy-start.3 = (f32[5,5,1,1024]{3,2,1,0:T(1,128)S(1)}, f32[5,5,1,1024]{3,2,1,0:T(1,128)}, u32[]{:S(2)}) copy-start(f32[5,5,1,1024]{3,2,1,0:T(1,128)} %copy-done.2) | copy-start | bytes 307204
Sparse Core Ops, SparseCore 0:
  12.2 62.6 all-gather.2

commit v5 on v4

--- a/solution.py
+++ b/solution.py
@@ -6,6 +6,7 @@
 from jax.sharding import PartitionSpec as P
 
 BLOCK_CELLS = 128
+HIGHEST = lax.Precision.HIGHEST
 
 
 def apply_block(matrix, vector):
@@ -14,26 +15,45 @@
 
 def chain_blocks(later, earlier):
     return jnp.sum(later[:, :, None] * earlier[None], axis=1)
+
+
+def owner_kernel(request_ref, table_ref, out_ref):
+    corners = request_ref.shape[0] // 2
+    rows = out_ref.shape[0]
+    blocks = table_ref.shape[0] // rows
+    chunk = 512
+    table = table_ref[...]
+    lanes = lax.broadcasted_iota(jnp.int32, (BLOCK_CELLS, chunk), 0).astype(jnp.float32)
+    for part in range(request_ref.shape[1] // chunk):
+        window = pl.ds(part * chunk, chunk)
+        wanted = request_ref[0:corners, window]
+        wts = request_ref[corners : 2 * corners, window]
+        block = jnp.floor(wanted[0:1] * (1.0 / BLOCK_CELLS))
+        spread = jnp.where(wanted[0:1] - block * BLOCK_CELLS == lanes, wts[0:1], 0.0)
+        for k in range(1, corners):
+            offs = wanted[k : k + 1] - block * BLOCK_CELLS
+            spread = spread + jnp.where(offs == lanes, wts[k : k + 1], 0.0)
+        every = jnp.dot(table, spread, precision=HIGHEST, preferred_element_type=jnp.float32)
+        total = jnp.where(block == 0.0, every[0:rows], 0.0)
+        for at in range(1, blocks):
+            total = total + jnp.where(block == float(at), every[at * rows : (at + 1) * rows], 0.0)
+        out_ref[:, window] = total
 
 
 def interpolate_at_owner(state_flat, request):
     width, resident = state_flat.shape
     blocks = resident // BLOCK_CELLS
-    corners = request.shape[0] // 2
-    wanted = request[:corners]
-    wts = request[corners:]
-    block = jnp.floor(wanted[0] * (1.0 / BLOCK_CELLS))
-    lanes = lax.broadcasted_iota(jnp.float32, (BLOCK_CELLS, 1), 0)
-    spread = jnp.zeros((BLOCK_CELLS, request.shape[1]), jnp.float32)
-    for k in range(corners):
-        offs = wanted[k] - block * BLOCK_CELLS
-        spread = spread + jnp.where(offs[None, :] == lanes, wts[k][None, :], 0.0)
     rows = 8
     table = state_flat.reshape(width, blocks, BLOCK_CELLS).transpose(1, 0, 2)
     table = jnp.pad(table, ((0, 0), (0, rows - width), (0, 0))).reshape(blocks * rows, BLOCK_CELLS)
-    every = jnp.dot(table, spread, precision=lax.Precision.HIGH).reshape(blocks, rows, -1)
-    ids = lax.broadcasted_iota(jnp.float32, (blocks, 1, 1), 0)
-    return jnp.sum(jnp.where(block[None, None, :] == ids, every, 0.0), axis=0)[:width]
+    vmem = pltpu.MemorySpace.VMEM
+    out = pl.pallas_call(
+        owner_kernel,
+        out_shape=jax.ShapeDtypeStruct((rows, request.shape[1]), jnp.float32),
+        in_specs=[pl.BlockSpec(memory_space=vmem), pl.BlockSpec(memory_space=vmem)],
+        out_specs=pl.BlockSpec(memory_space=vmem),
+    )(request, table)
+    return out[:width]
 
 
 def fold_kernel(index_ref, maps_ref, offsets_ref, out_ref, up_ref):

time: 111 us -> 111 us (level)
  Pallas kernels: 4.99 us -> 9.77 us
  matrix products: 2.89 us -> 0 us
  local copies, waits for them, and re-layouts: 23.7 us -> 22.5 us
    pallas_call x0 -> x1, Pallas kernels: none -> 4.79 us  [interpolate_at_owner(): pl.pallas_call(owner_kernel, out_shape=jax.ShapeDtypeStruct((rows, reques...]
    slice x1 -> x0, local copies, waits for them, and re-layouts: 2.99 us -> none  [interpolate_at_owner(): spread = spread + jnp.where(offs[None, :] == lanes, wts[k][None, :], 0.0)]
    dot_general x1 -> x0, matrix products: 2.89 us -> none  [interpolate_at_owner(): jnp.dot(table, spread, precision=lax.Precision.HIGH)]
    reshape x0 -> x2, local copies, waits for them, and re-layouts: none -> 1.82 us  [the longest x1 1.19 us: sweep_body(): received.reshape(received.shape[0], -1)]
    unnamed x35 -> x37, local copies, waits for them, and re-layouts: 2.63 us -> 2.63 us
  transfers between devices with their start and end apart: 4 -> 4, of which waited for: 3 -> 3; matrix products, arithmetic and copies ran while one was open for 25% -> 20% of each run, Pallas kernels for 0% -> 4%
where the time goes in v5:
time: 111 us
  waiting for transfers between devices  38 us (34%)
  local copies, waits for them, and re-layouts  22.5 us (20%)
  starting transfers between devices  20 us (18%)
  between operations  14.1 us (13%)
  Pallas kernels  9.77 us (9%)
  other arithmetic  6.44 us (6%)
    all_to_all x1, waiting for transfers between devices, sweep_body(): every = lax.all_to_all(spread, 'slab', 0, 0, tiled=True)  20.6 us
    all_to_all x1, starting transfers between devices, sweep_body(): lax.all_to_all(request, ('slab', 'cross'), split_axis=1, concat_axis=1, t...  11.2 us
    all_to_all x1, waiting for transfers between devices, sweep_body(): lax.all_to_all(answer, ('slab', 'cross'), split_axis=1, concat_axis=1, ti...  9.39 us
    all_to_all x1, waiting for transfers between devices, sweep_body(): lax.all_to_all(request, ('slab', 'cross'), split_axis=1, concat_axis=1, t...  8.08 us
    pallas_call x1, Pallas kernels, fold_entries(): pl.pallas_call(fold_kernel, out_shape=jax.ShapeDtypeStruct((2, width, sub...  4.99 us
    all_to_all x1, starting transfers between devices, sweep_body(): lax.all_to_all(answer, ('slab', 'cross'), split_axis=1, concat_axis=1, ti...  4.86 us
    pallas_call x1, Pallas kernels, interpolate_at_owner(): pl.pallas_call(owner_kernel, out_shape=jax.ShapeDtypeStruct((rows, reques...  4.79 us
    all_to_all x1, starting transfers between devices, sweep_body(): every = lax.all_to_all(spread, 'slab', 0, 0, tiled=True)  3.95 us
  transfers between devices with their start and end apart: 4, of which 3 were waited for; matrix products, arithmetic and copies ran while one was open for 20% of the time, Pallas kernels for 4%

profile of v5, /device:TPU:0, one launch (start us, length us, event | category | flops | bytes accessed | tf_op | source)
XLA Modules:
  0.0 110.8 jit_solution(8353873572549030296)
XLA Ops:
  6.5 1.2 %fusion.7 = (f32[5,5,1,1024]{3,2,1,0:T(1,128)S(1)}, f32[5,5,1,1024]{3,2,1,0:T(1,128)S(1)}) fusion(f32[5,5,2,1024]{3,2,1,0:T(2,128)} %param.13), kind=kLoop, calls=%fused_computation.74 | loop fusion | bytes 409600 | tf_op jit(solution)/shard_map/slice | solution.py:138
  7.8 1.3 %fusion.9 = (f32[5,5,1,1024]{3,2,1,0:T(1,128)S(1)}, f32[5,5,1,1024]{3,2,1,0:T(1,128)S(1)}) fusion(f32[5,5,2,1024]{3,2,1,0:T(2,128)} %param.12), kind=kLoop, calls=%fused_computation.76 | loop fusion | bytes 409600 | tf_op jit(solution)/shard_map/slice | solution.py:209
  9.1 1.2 %fusion.8 = (f32[5,5,1,1024]{3,2,1,0:T(1,128)S(1)}, f32[5,5,1,1024]{3,2,1,0:T(1,128)S(1)}) fusion(f32[5,5,2,1024]{3,2,1,0:T(2,128)} %param.14), kind=kLoop, calls=%fused_computation.75 | loop fusion | bytes 409600 | tf_op jit(solution)/shard_map/slice | solution.py:142
  11.3 0.8 pad_maximum_fusion
  12.9 0.4 fusion.2
  13.2 0.5 and_reduce_fusion
  13.8 3.6 %scatter_custom_fusion = f32[16,4096]{0,1:T(8,128)S(1)} fusion(s32[1024]{0:T(1024)S(1)} %bitcast.135, f32[1024,16]{1,0:T(8,128)S(1)} %copy.68, f32[]{:T(128)} %constant.38.clone.1), kind=kCustom, calls=%fused_computation.2 | custom fusion | bytes 262148 | tf_op jit(solution)/shard_map/scatter | solution.py:163
  17.4 0.6 copy.69
  18.0 1.2 %reshape.241 = f32[128,1,512]{2,1,0:T(1,128)} reshape(f32[128,16,32]{2,1,0:T(8,128)S(1)} %bitcast.121) | data formatting | bytes 524288
  19.2 11.2 %all-to-all-start = ((f32[128,1,512]{2,1,0:T(1,128)}), f32[128,1,512]{2,1,0:T(1,128)S(1)}, u32[]{:S(2)}, u32[]{:S(2)}) async-start(f32[128,1,512]{2,1,0:T(1,128)} %reshape.241), calls=%async_computation | async-start | bytes 524288 | tf_op jit(solution)/shard_map/all_to_all | solution.py:164
  30.3 0.8 reshape_reshape.4
  31.2 0.7 slice_bitcast_fusion.3
  32.2 0.6 pad_bitcast_fusion.table_ref
  32.9 8.1 %all-to-all-done = f32[128,1,512]{2,1,0:T(1,128)S(1)} async-done(((f32[128,1,512]{2,1,0:T(1,128)}), f32[128,1,512]{2,1,0:T(1,128)S(1)}, u32[]{:S(2)}, u32[]{:S(2)}) %all-to-all-start) | async-done | bytes 262176 | tf_op jit(solution)/shard_map/all_to_all | solution.py:164
  41.0 0.5 broadcast.95
  41.5 1.3 %reduce.2 = f32[128,512]{1,0:T(8,128)S(1)} reduce(f32[128,1,512]{2,1,0:T(1,128)S(1)} %all-to-all-done, f32[]{:T(128)} %broadcast.95), dimensions={1}, to_apply=%all_to_all.9.reduce_sub_computation | reduce | bytes 524292 | tf_op jit(solution)/shard_map/all_to_all | solution.py:164
  42.8 0.3 reshape.242
  43.1 0.3 copy.70
  43.4 1.2 %reshape.213.request_ref = f32[16,4096]{1,0:T(8,128)} reshape(f32[16,128,32]{2,1,0:T(8,128)S(1)} %copy.70) | data formatting | bytes 524288 | tf_op jit(solution)/shard_map/reshape | solution.py:165
  44.6 4.8 %shard_map.100 = f32[8,4096]{1,0:T(8,128)} custom-call(f32[16,4096]{1,0:T(8,128)} %reshape.213.request_ref, f32[128,128]{1,0:T(8,128)} %pad_bitcast_fusion.table_ref), custom_call_target="tpu_custom_call" | custom-call | tf_op jit(solution)/shard_map/pallas_call | solution.py:50
  49.4 1.0 reshape.215
  50.6 0.9 reshape.243
  51.5 4.9 %all-to-all-start.1 = ((f32[128,1,160]{2,1,0:T(1,128)}), f32[128,1,160]{2,1,0:T(1,128)S(1)}, u32[]{:S(2)}, u32[]{:S(2)}) async-start(f32[128,1,160]{2,1,0:T(1,128)} %reshape.243), calls=%async_computation.1 | async-start | bytes 262144 | tf_op jit(solution)/shard_map/all_to_all | solution.py:167
  56.5 9.4 %all-to-all-done.1 = f32[128,1,160]{2,1,0:T(1,128)S(1)} async-done(((f32[128,1,160]{2,1,0:T(1,128)}), f32[128,1,160]{2,1,0:T(1,128)S(1)}, u32[]{:S(2)}, u32[]{:S(2)}) %all-to-all-start.1) | async-done | bytes 81952 | tf_op jit(solution)/shard_map/all_to_all | solution.py:167
  65.9 1.0 reduce.3
  67.0 0.8 copy.73
  67.8 2.8 %gather_fusion = f32[1024,5]{1,0:T(8,128)S(1)} fusion(f32[5,4096]{0,1:T(8,128)S(1)} %bitcast.123, s32[1024]{0:T(1024)S(1)} %broadcast_clamp_fusion), kind=kCustom, calls=%fused_computation | custom fusion | bytes 45056 | tf_op jit(solution)/shard_map/jit(_take)/gather | solution.py:168
  71.9 1.2 %broadcast_in_dim.92 = f32[32,2,5,8,128]{4,3,2,1,0:T(8,128)} broadcast(f32[2,5,8,128]{3,2,1,0:T(8,128)S(1)} %maximum_bitcast_fusion.1), dimensions={1,2,3,4} | broadcast | bytes 1351680 | tf_op jit(solution)/shard_map/broadcast_in_dim | solution.py:196
  73.1 4.0 %all-to-all-start.2 = ((f32[32,2,5,8,128]{4,3,2,1,0:T(8,128)}), f32[32,2,5,8,128]{4,3,2,1,0:T(8,128)S(1)}, u32[]{:S(2)}, u32[]{:S(2)}) async-start(f32[32,2,5,8,128]{4,3,2,1,0:T(8,128)} %broadcast_in_dim.92), calls=%async_computation.2 | async-start | bytes 2621440 | tf_op jit(solution)/shard_map/all_to_all | solution.py:197
  77.0 20.6 %all-to-all-done.2 = f32[32,2,5,8,128]{4,3,2,1,0:T(8,128)S(1)} async-done(((f32[32,2,5,8,128]{4,3,2,1,0:T(8,128)}), f32[32,2,5,8,128]{4,3,2,1,0:T(8,128)S(1)}, u32[]{:S(2)}, u32[]{:S(2)}) %all-to-all-start.2) | async-done | bytes 1310752 | tf_op jit(solution)/shard_map/all_to_all | solution.py:197
  97.6 5.0 %shard_map.101 = f32[2,5,8,128]{3,2,1,0:T(8,128)S(1)} custom-call(s32[1]{0:T(128)} %bitcast.17.index_ref, f32[32,75,8,128]{3,2,1,0:T(8,128)} %bitcast.119, f32[32,10,8,128]{3,2,1,0:T(8,128)S(1)} %bitcast.118), custom_call_target="tpu_custom_call" | custom-call | tf_op jit(solution)/shard_map/pallas_call | solution.py:108
  103.3 0.7 copy.80
  (97 shorter events, 4.2 us)
Async XLA Ops:
  6.5 91.1 %all-gather.3.cloned.1.call-start = ((), (), s32[]{:S(2)}) async-start(), calls=%async_computation.3 | async-start | bytes 10137600 | tf_op jit(solution)/shard_map/all_gather | solution.py:153
  7.7 2.7 %copy-start = (f32[5,5,1,1024]{3,2,1,0:T(1,128)}, f32[5,5,1,1024]{3,2,1,0:T(1,128)S(1)}, u32[]{:S(2)}) copy-start(f32[5,5,1,1024]{3,2,1,0:T(1,128)S(1)} %get-tuple-element.17) | copy-start | bytes 307204
  7.8 2.7 %copy-start.2 = (f32[5,5,1,1024]{3,2,1,0:T(1,128)}, f32[5,5,1,1024]{3,2,1,0:T(1,128)S(1)}, u32[]{:S(2)}) copy-start(f32[5,5,1,1024]{3,2,1,0:T(1,128)S(1)} %get-tuple-element.18) | copy-start | bytes 307204
  10.7 1.4 %copy-start.7 = (s32[1024,1]{0,1:T(1,128)S(1)}, s32[1024,1]{0,1:T(1,128)}, u32[]{:S(2)}) copy-start(s32[1024,1]{0,1:T(1,128)} %param.15) | copy-start | bytes 12292
  11.2 1.4 %copy-start.13 = (s32[1024]{0:T(1024)S(1)}, s32[1024]{0:T(1024)}, u32[]{:S(2)}) copy-start(s32[1024]{0:T(1024)} %param.16) | copy-start | bytes 12292
  11.2 1.4 %copy-start.8 = (s32[8,1024]{1,0:T(8,128)S(1)}, s32[8,1024]{1,0:T(8,128)}, u32[]{:S(2)}) copy-start(s32[8,1024]{1,0:T(8,128)} %param.17) | copy-start | bytes 98308
  11.2 1.4 %copy-start.9 = (f32[8,1024]{1,0:T(8,128)S(1)}, f32[8,1024]{1,0:T(8,128)}, u32[]{:S(2)}) copy-start(f32[8,1024]{1,0:T(8,128)} %param.18) | copy-start | bytes 98308
  13.8 3.6 %copy-start.10 = (s32[1024,1]{0,1:T(1,128)}, s32[1024,1]{0,1:T(1,128)S(1)}, u32[]{:S(2)}) copy-start(s32[1024,1]{0,1:T(1,128)S(1)} %get-tuple-element.16) | copy-start | bytes 12292
  18.0 14.0 %copy-start.3 = (f32[5,5,1,1024]{3,2,1,0:T(1,128)S(1)}, f32[5,5,1,1024]{3,2,1,0:T(1,128)}, u32[]{:S(2)}) copy-start(f32[5,5,1,1024]{3,2,1,0:T(1,128)} %copy-done.2) | copy-start | bytes 307204
  18.0 14.9 %copy-start.11 = (s32[1024,1]{0,1:T(1,128)S(1)}, s32[1024,1]{0,1:T(1,128)}, u32[]{:S(2)}) copy-start(s32[1024,1]{0,1:T(1,128)} %copy-done.10) | copy-start | bytes 12292
  19.2 21.8 %all-to-all-start = ((f32[128,1,512]{2,1,0:T(1,128)}), f32[128,1,512]{2,1,0:T(1,128)S(1)}, u32[]{:S(2)}, u32[]{:S(2)}) async-start(f32[128,1,512]{2,1,0:T(1,128)} %reshape.241), calls=%async_computation | async-start | bytes 524288 | tf_op jit(solution)/shard_map/all_to_all | solution.py:164
  51.5 19.1 %copy-start.12 = (pred[1024]{0:T(1024)(128)(4,1)S(1)}, pred[1024]{0:T(1024)(128)(4,1)}, u32[]{:S(2)}) copy-start(pred[1024]{0:T(1024)(128)(4,1)} %get-tuple-element.15) | copy-start | bytes 3076
  51.5 14.3 %all-to-all-start.1 = ((f32[128,1,160]{2,1,0:T(1,128)}), f32[128,1,160]{2,1,0:T(1,128)S(1)}, u32[]{:S(2)}, u32[]{:S(2)}) async-start(f32[128,1,160]{2,1,0:T(1,128)} %reshape.243), calls=%async_computation.1 | async-start | bytes 262144 | tf_op jit(solution)/shard_map/all_to_all | solution.py:167
  67.0 4.3 %copy-start.5 = (f32[5,2,1024]{2,1,0:T(2,128)S(1)}, f32[5,2,1024]{2,1,0:T(2,128)}, u32[]{:S(2)}) copy-start(f32[5,2,1024]{2,1,0:T(2,128)} %param.10) | copy-start | bytes 122884
  67.0 4.3 %copy-start.6 = (f32[5,2,1024]{2,1,0:T(2,128)S(1)}, f32[5,2,1024]{2,1,0:T(2,128)}, u32[]{:S(2)}) copy-start(f32[5,2,1024]{2,1,0:T(2,128)} %param.11) | copy-start | bytes 122884
  67.0 4.5 %copy-start.1 = (f32[5,5,1,1024]{3,2,1,0:T(1,128)S(1)}, f32[5,5,1,1024]{3,2,1,0:T(1,128)}, u32[]{:S(2)}) copy-start(f32[5,5,1,1024]{3,2,1,0:T(1,128)} %copy-done) | copy-start | bytes 307204
  73.1 24.5 %all-to-all-start.2 = ((f32[32,2,5,8,128]{4,3,2,1,0:T(8,128)}), f32[32,2,5,8,128]{4,3,2,1,0:T(8,128)S(1)}, u32[]{:S(2)}, u32[]{:S(2)}) async-start(f32[32,2,5,8,128]{4,3,2,1,0:T(8,128)} %broadcast_in_dim.92), calls=%async_computation.2 | async-start | bytes 2621440 | tf_op jit(solution)/shard_map/all_to_all | solution.py:197
  97.6 5.0 %copy-start.4 = (f32[5,5,1,1024]{3,2,1,0:T(1,128)S(1)}, f32[5,5,1,1024]{3,2,1,0:T(1,128)}, u32[]{:S(2)}) copy-start(f32[5,5,1,1024]{3,2,1,0:T(1,128)} %copy-done.2) | copy-start | bytes 307204
Sparse Core Ops, SparseCore 0:
  12.2 62.6 all-gather.2

commit v6 on v5

--- a/solution.py
+++ b/solution.py
@@ -56,12 +56,18 @@
     return out[:width]
 
 
-def fold_kernel(index_ref, maps_ref, offsets_ref, out_ref, up_ref):
+def fold_kernel(index_ref, maps_hbm, offsets_ref, out_ref, up_ref, maps_ref, arrived):
     peers = maps_ref.shape[0]
     width = out_ref.shape[1]
     square = width * width
     here = index_ref[0]
     zero = offsets_ref[0, 0] * 0.0
+
+    def copy(at):
+        return pltpu.make_async_copy(maps_hbm.at[at], maps_ref.at[at], arrived.at[at])
+
+    for at in range(peers):
+        copy(at).start()
 
     def matvec(at, base, vector):
         rows = []
@@ -73,6 +79,7 @@
         return rows
 
     def lower_step(at, carry):
+        copy(at).wait()
         entry, kept = carry
         hit = at == here
         kept = tuple(jnp.where(hit, e, k) for e, k in zip(entry, kept))
@@ -84,7 +91,7 @@
         return entry, kept
 
     start = (tuple([zero] * width), tuple([zero] * width))
-    _, low = lax.fori_loop(0, peers, lower_step, start)
+    _, low = lax.fori_loop(0, peers, lower_step, start, unroll=True)
 
     def upper_step(step, carry):
         at = peers - 1 - step
@@ -95,7 +102,7 @@
         entry = tuple(moved[i] + up_ref[at, i] for i in range(width))
         return entry, kept
 
-    _, up = lax.fori_loop(0, peers, upper_step, start)
+    _, up = lax.fori_loop(0, peers, upper_step, start, unroll=True)
     for i in range(width):
         out_ref[0, i] = low[i]
         out_ref[1, i] = up[i]
@@ -110,11 +117,15 @@
         out_shape=jax.ShapeDtypeStruct((2, width, sub, lanes), jnp.float32),
         in_specs=[
             pl.BlockSpec(memory_space=pltpu.MemorySpace.SMEM),
-            pl.BlockSpec(memory_space=vmem),
+            pl.BlockSpec(memory_space=pl.ANY),
             pl.BlockSpec(memory_space=vmem),
         ],
         out_specs=pl.BlockSpec(memory_space=vmem),
-        scratch_shapes=[pltpu.VMEM((peers, width, sub, lanes), jnp.float32)],
+        scratch_shapes=[
+            pltpu.VMEM((peers, width, sub, lanes), jnp.float32),
+            pltpu.VMEM(all_maps.shape, jnp.float32),
+            pltpu.SemaphoreType.DMA((peers,)),
+        ],
         compiler_params=pltpu.CompilerParams(vmem_limit_bytes=48 * 1024 * 1024),
     )(index, all_maps, every)
 

time: 111 us -> 111 us (level)
  no operation moved by 1% of the time
where the time goes in v6:
time: 111 us; the launch traced here: 110 us
  waiting for transfers between devices  38 us (34%)
  local copies, waits for them, and re-layouts  22.5 us (20%)
  starting transfers between devices  20 us (18%)
  between operations  14.1 us (13%)
  Pallas kernels  9.13 us (8%)
  other arithmetic  6.44 us (6%)
    all_to_all x1, waiting for transfers between devices, sweep_body(): every = lax.all_to_all(spread, 'slab', 0, 0, tiled=True)  20.6 us
    all_to_all x1, starting transfers between devices, sweep_body(): lax.all_to_all(request, ('slab', 'cross'), split_axis=1, concat_axis=1, t...  11.2 us
    all_to_all x1, waiting for transfers between devices, sweep_body(): lax.all_to_all(answer, ('slab', 'cross'), split_axis=1, concat_axis=1, ti...  9.39 us
    all_to_all x1, waiting for transfers between devices, sweep_body(): lax.all_to_all(request, ('slab', 'cross'), split_axis=1, concat_axis=1, t...  8.08 us
    all_to_all x1, starting transfers between devices, sweep_body(): lax.all_to_all(answer, ('slab', 'cross'), split_axis=1, concat_axis=1, ti...  4.86 us
    pallas_call x1, Pallas kernels, interpolate_at_owner(): pl.pallas_call(owner_kernel, out_shape=jax.ShapeDtypeStruct((rows, reques...  4.79 us
    pallas_call x1, Pallas kernels, fold_entries(): pl.pallas_call(fold_kernel, out_shape=jax.ShapeDtypeStruct((2, width, sub...  4.34 us
    all_to_all x1, starting transfers between devices, sweep_body(): every = lax.all_to_all(spread, 'slab', 0, 0, tiled=True)  3.95 us
  transfers between devices with their start and end apart: 4, of which 3 were waited for; matrix products, arithmetic and copies ran while one was open for 20% of the time, Pallas kernels for 4%

profile of v6, /device:TPU:0, one launch (start us, length us, event | category | flops | bytes accessed | tf_op | source)
XLA Modules:
  0.0 110.2 jit_solution(15017130165640355745)
XLA Ops:
  6.5 1.2 %fusion.7 = (f32[5,5,1,1024]{3,2,1,0:T(1,128)S(1)}, f32[5,5,1,1024]{3,2,1,0:T(1,128)S(1)}) fusion(f32[5,5,2,1024]{3,2,1,0:T(2,128)} %param.13), kind=kLoop, calls=%fused_computation.74 | loop fusion | bytes 409600 | tf_op jit(solution)/shard_map/slice | solution.py:149
  7.8 1.3 %fusion.9 = (f32[5,5,1,1024]{3,2,1,0:T(1,128)S(1)}, f32[5,5,1,1024]{3,2,1,0:T(1,128)S(1)}) fusion(f32[5,5,2,1024]{3,2,1,0:T(2,128)} %param.12), kind=kLoop, calls=%fused_computation.76 | loop fusion | bytes 409600 | tf_op jit(solution)/shard_map/slice | solution.py:220
  9.1 1.2 %fusion.8 = (f32[5,5,1,1024]{3,2,1,0:T(1,128)S(1)}, f32[5,5,1,1024]{3,2,1,0:T(1,128)S(1)}) fusion(f32[5,5,2,1024]{3,2,1,0:T(2,128)} %param.14), kind=kLoop, calls=%fused_computation.75 | loop fusion | bytes 409600 | tf_op jit(solution)/shard_map/slice | solution.py:153
  11.3 0.8 pad_maximum_fusion
  12.9 0.4 fusion.2
  13.2 0.5 and_reduce_fusion
  13.8 3.6 %scatter_custom_fusion = f32[16,4096]{0,1:T(8,128)S(1)} fusion(s32[1024]{0:T(1024)S(1)} %bitcast.135, f32[1024,16]{1,0:T(8,128)S(1)} %copy.68, f32[]{:T(128)} %constant.38.clone.1), kind=kCustom, calls=%fused_computation.2 | custom fusion | bytes 262148 | tf_op jit(solution)/shard_map/scatter | solution.py:174
  17.4 0.6 copy.69
  18.0 1.2 %reshape.241 = f32[128,1,512]{2,1,0:T(1,128)} reshape(f32[128,16,32]{2,1,0:T(8,128)S(1)} %bitcast.121) | data formatting | bytes 524288
  19.2 11.2 %all-to-all-start = ((f32[128,1,512]{2,1,0:T(1,128)}), f32[128,1,512]{2,1,0:T(1,128)S(1)}, u32[]{:S(2)}, u32[]{:S(2)}) async-start(f32[128,1,512]{2,1,0:T(1,128)} %reshape.241), calls=%async_computation | async-start | bytes 524288 | tf_op jit(solution)/shard_map/all_to_all | solution.py:175
  30.3 0.8 reshape_reshape.4
  31.2 0.7 slice_bitcast_fusion.3
  32.2 0.6 pad_bitcast_fusion.table_ref
  32.9 8.1 %all-to-all-done = f32[128,1,512]{2,1,0:T(1,128)S(1)} async-done(((f32[128,1,512]{2,1,0:T(1,128)}), f32[128,1,512]{2,1,0:T(1,128)S(1)}, u32[]{:S(2)}, u32[]{:S(2)}) %all-to-all-start) | async-done | bytes 262176 | tf_op jit(solution)/shard_map/all_to_all | solution.py:175
  41.0 0.5 broadcast.95
  41.5 1.3 %reduce.2 = f32[128,512]{1,0:T(8,128)S(1)} reduce(f32[128,1,512]{2,1,0:T(1,128)S(1)} %all-to-all-done, f32[]{:T(128)} %broadcast.95), dimensions={1}, to_apply=%all_to_all.9.reduce_sub_computation | reduce | bytes 524292 | tf_op jit(solution)/shard_map/all_to_all | solution.py:175
  42.8 0.3 reshape.242
  43.1 0.3 copy.70
  43.4 1.2 %reshape.213.request_ref = f32[16,4096]{1,0:T(8,128)} reshape(f32[16,128,32]{2,1,0:T(8,128)S(1)} %copy.70) | data formatting | bytes 524288 | tf_op jit(solution)/shard_map/reshape | solution.py:176
  44.6 4.8 %shard_map.100 = f32[8,4096]{1,0:T(8,128)} custom-call(f32[16,4096]{1,0:T(8,128)} %reshape.213.request_ref, f32[128,128]{1,0:T(8,128)} %pad_bitcast_fusion.table_ref), custom_call_target="tpu_custom_call" | custom-call | tf_op jit(solution)/shard_map/pallas_call | solution.py:50
  49.4 1.0 reshape.215
  50.6 0.9 reshape.243
  51.5 4.9 %all-to-all-start.1 = ((f32[128,1,160]{2,1,0:T(1,128)}), f32[128,1,160]{2,1,0:T(1,128)S(1)}, u32[]{:S(2)}, u32[]{:S(2)}) async-start(f32[128,1,160]{2,1,0:T(1,128)} %reshape.243), calls=%async_computation.1 | async-start | bytes 262144 | tf_op jit(solution)/shard_map/all_to_all | solution.py:178
  56.5 9.4 %all-to-all-done.1 = f32[128,1,160]{2,1,0:T(1,128)S(1)} async-done(((f32[128,1,160]{2,1,0:T(1,128)}), f32[128,1,160]{2,1,0:T(1,128)S(1)}, u32[]{:S(2)}, u32[]{:S(2)}) %all-to-all-start.1) | async-done | bytes 81952 | tf_op jit(solution)/shard_map/all_to_all | solution.py:178
  65.9 1.0 reduce.3
  67.0 0.8 copy.73
  67.8 2.8 %gather_fusion = f32[1024,5]{1,0:T(8,128)S(1)} fusion(f32[5,4096]{0,1:T(8,128)S(1)} %bitcast.123, s32[1024]{0:T(1024)S(1)} %broadcast_clamp_fusion), kind=kCustom, calls=%fused_computation | custom fusion | bytes 45056 | tf_op jit(solution)/shard_map/jit(_take)/gather | solution.py:179
  71.9 1.2 %broadcast_in_dim.92 = f32[32,2,5,8,128]{4,3,2,1,0:T(8,128)} broadcast(f32[2,5,8,128]{3,2,1,0:T(8,128)S(1)} %maximum_bitcast_fusion.1), dimensions={1,2,3,4} | broadcast | bytes 1351680 | tf_op jit(solution)/shard_map/broadcast_in_dim | solution.py:207
  73.1 4.0 %all-to-all-start.2 = ((f32[32,2,5,8,128]{4,3,2,1,0:T(8,128)}), f32[32,2,5,8,128]{4,3,2,1,0:T(8,128)S(1)}, u32[]{:S(2)}, u32[]{:S(2)}) async-start(f32[32,2,5,8,128]{4,3,2,1,0:T(8,128)} %broadcast_in_dim.92), calls=%async_computation.2 | async-start | bytes 2621440 | tf_op jit(solution)/shard_map/all_to_all | solution.py:208
  77.0 20.6 %all-to-all-done.2 = f32[32,2,5,8,128]{4,3,2,1,0:T(8,128)S(1)} async-done(((f32[32,2,5,8,128]{4,3,2,1,0:T(8,128)}), f32[32,2,5,8,128]{4,3,2,1,0:T(8,128)S(1)}, u32[]{:S(2)}, u32[]{:S(2)}) %all-to-all-start.2) | async-done | bytes 1310752 | tf_op jit(solution)/shard_map/all_to_all | solution.py:208
  97.6 4.3 %shard_map.101 = f32[2,5,8,128]{3,2,1,0:T(8,128)S(1)} custom-call(s32[1]{0:T(128)} %bitcast.17.index_ref, f32[32,75,8,128]{3,2,1,0:T(8,128)} %bitcast.119, f32[32,10,8,128]{3,2,1,0:T(8,128)S(1)} %bitcast.118), custom_call_target="tpu_custom_call" | custom-call | tf_op jit(solution)/shard_map/pallas_call | solution.py:115
  102.7 0.7 copy.80
  (97 shorter events, 4.2 us)
Async XLA Ops:
  6.5 91.1 %all-gather.3.cloned.1.call-start = ((), (), s32[]{:S(2)}) async-start(), calls=%async_computation.3 | async-start | bytes 10137600 | tf_op jit(solution)/shard_map/all_gather | solution.py:164
  7.7 2.7 %copy-start = (f32[5,5,1,1024]{3,2,1,0:T(1,128)}, f32[5,5,1,1024]{3,2,1,0:T(1,128)S(1)}, u32[]{:S(2)}) copy-start(f32[5,5,1,1024]{3,2,1,0:T(1,128)S(1)} %get-tuple-element.17) | copy-start | bytes 307204
  7.8 2.7 %copy-start.2 = (f32[5,5,1,1024]{3,2,1,0:T(1,128)}, f32[5,5,1,1024]{3,2,1,0:T(1,128)S(1)}, u32[]{:S(2)}) copy-start(f32[5,5,1,1024]{3,2,1,0:T(1,128)S(1)} %get-tuple-element.18) | copy-start | bytes 307204
  10.7 1.4 %copy-start.7 = (s32[1024,1]{0,1:T(1,128)S(1)}, s32[1024,1]{0,1:T(1,128)}, u32[]{:S(2)}) copy-start(s32[1024,1]{0,1:T(1,128)} %param.15) | copy-start | bytes 12292
  11.2 1.4 %copy-start.13 = (s32[1024]{0:T(1024)S(1)}, s32[1024]{0:T(1024)}, u32[]{:S(2)}) copy-start(s32[1024]{0:T(1024)} %param.16) | copy-start | bytes 12292
  11.2 1.4 %copy-start.8 = (s32[8,1024]{1,0:T(8,128)S(1)}, s32[8,1024]{1,0:T(8,128)}, u32[]{:S(2)}) copy-start(s32[8,1024]{1,0:T(8,128)} %param.17) | copy-start | bytes 98308
  11.2 1.4 %copy-start.9 = (f32[8,1024]{1,0:T(8,128)S(1)}, f32[8,1024]{1,0:T(8,128)}, u32[]{:S(2)}) copy-start(f32[8,1024]{1,0:T(8,128)} %param.18) | copy-start | bytes 98308
  13.8 3.6 %copy-start.10 = (s32[1024,1]{0,1:T(1,128)}, s32[1024,1]{0,1:T(1,128)S(1)}, u32[]{:S(2)}) copy-start(s32[1024,1]{0,1:T(1,128)S(1)} %get-tuple-element.16) | copy-start | bytes 12292
  18.0 14.0 %copy-start.3 = (f32[5,5,1,1024]{3,2,1,0:T(1,128)S(1)}, f32[5,5,1,1024]{3,2,1,0:T(1,128)}, u32[]{:S(2)}) copy-start(f32[5,5,1,1024]{3,2,1,0:T(1,128)} %copy-done.2) | copy-start | bytes 307204
  18.0 14.9 %copy-start.11 = (s32[1024,1]{0,1:T(1,128)S(1)}, s32[1024,1]{0,1:T(1,128)}, u32[]{:S(2)}) copy-start(s32[1024,1]{0,1:T(1,128)} %copy-done.10) | copy-start | bytes 12292
  19.2 21.8 %all-to-all-start = ((f32[128,1,512]{2,1,0:T(1,128)}), f32[128,1,512]{2,1,0:T(1,128)S(1)}, u32[]{:S(2)}, u32[]{:S(2)}) async-start(f32[128,1,512]{2,1,0:T(1,128)} %reshape.241), calls=%async_computation | async-start | bytes 524288 | tf_op jit(solution)/shard_map/all_to_all | solution.py:175
  51.5 19.1 %copy-start.12 = (pred[1024]{0:T(1024)(128)(4,1)S(1)}, pred[1024]{0:T(1024)(128)(4,1)}, u32[]{:S(2)}) copy-start(pred[1024]{0:T(1024)(128)(4,1)} %get-tuple-element.15) | copy-start | bytes 3076
  51.5 14.3 %all-to-all-start.1 = ((f32[128,1,160]{2,1,0:T(1,128)}), f32[128,1,160]{2,1,0:T(1,128)S(1)}, u32[]{:S(2)}, u32[]{:S(2)}) async-start(f32[128,1,160]{2,1,0:T(1,128)} %reshape.243), calls=%async_computation.1 | async-start | bytes 262144 | tf_op jit(solution)/shard_map/all_to_all | solution.py:178
  67.0 4.3 %copy-start.5 = (f32[5,2,1024]{2,1,0:T(2,128)S(1)}, f32[5,2,1024]{2,1,0:T(2,128)}, u32[]{:S(2)}) copy-start(f32[5,2,1024]{2,1,0:T(2,128)} %param.10) | copy-start | bytes 122884
  67.0 4.3 %copy-start.6 = (f32[5,2,1024]{2,1,0:T(2,128)S(1)}, f32[5,2,1024]{2,1,0:T(2,128)}, u32[]{:S(2)}) copy-start(f32[5,2,1024]{2,1,0:T(2,128)} %param.11) | copy-start | bytes 122884
  67.0 4.5 %copy-start.1 = (f32[5,5,1,1024]{3,2,1,0:T(1,128)S(1)}, f32[5,5,1,1024]{3,2,1,0:T(1,128)}, u32[]{:S(2)}) copy-start(f32[5,5,1,1024]{3,2,1,0:T(1,128)} %copy-done) | copy-start | bytes 307204
  73.1 24.5 %all-to-all-start.2 = ((f32[32,2,5,8,128]{4,3,2,1,0:T(8,128)}), f32[32,2,5,8,128]{4,3,2,1,0:T(8,128)S(1)}, u32[]{:S(2)}, u32[]{:S(2)}) async-start(f32[32,2,5,8,128]{4,3,2,1,0:T(8,128)} %broadcast_in_dim.92), calls=%async_computation.2 | async-start | bytes 2621440 | tf_op jit(solution)/shard_map/all_to_all | solution.py:208
  97.6 4.4 %copy-start.4 = (f32[5,5,1,1024]{3,2,1,0:T(1,128)S(1)}, f32[5,5,1,1024]{3,2,1,0:T(1,128)}, u32[]{:S(2)}) copy-start(f32[5,5,1,1024]{3,2,1,0:T(1,128)} %copy-done.2) | copy-start | bytes 307204
Sparse Core Ops, SparseCore 0:
  12.2 62.6 all-gather.2

commit v7 on v6

--- a/solution.py
+++ b/solution.py
@@ -143,21 +143,27 @@
     blocks = resident_cells // BLOCK_CELLS
     square = width * width
 
+    tile = (cells // BLOCK_CELLS, BLOCK_CELLS)
+    tiled_dinv = dinv.reshape((width, width, planes) + tile)
+    tiled_lower = lower_jac.reshape((width, width, planes) + tile)
+    tiled_upper = upper_jac.reshape((width, width, planes) + tile)
     partial = []
     transfer = None
     for index in range(planes):
-        step = chain_blocks(dinv[:, :, index], lower_jac[:, :, index])
+        step = chain_blocks(tiled_dinv[:, :, index], tiled_lower[:, :, index])
         transfer = step if transfer is None else chain_blocks(step, transfer)
         partial.append(transfer)
     low_map = transfer
-    up_steps = [chain_blocks(dinv[:, :, index], upper_jac[:, :, index]) for index in range(planes)]
+    up_steps = [
+        chain_blocks(tiled_dinv[:, :, index], tiled_upper[:, :, index])
+        for index in range(planes)
+    ]
     up_map = None
     response = partial[planes - 1]
     for index in range(planes - 1, -1, -1):
         up_map = up_steps[index] if up_map is None else chain_blocks(up_steps[index], up_map)
         if index < planes - 1:
             response = partial[index] + chain_blocks(up_steps[index], response)
-    tile = (cells // BLOCK_CELLS, BLOCK_CELLS)
     maps = jnp.concatenate(
         [m.reshape((square,) + tile) for m in (low_map, up_map, response)], axis=0
     )

time: 111 us -> 109 us (0.982)
  local copies, waits for them, and re-layouts: 22.5 us -> 20.9 us
    reshape x2 -> x3, local copies, waits for them, and re-layouts: 0.06 us -> 3.29 us  [the longest x1 1.1 us: sweep_body(): tiled_dinv = dinv.reshape((width, width, planes) + tile)]
    slice x1, local copies, waits for them, and re-layouts: 1.28 us -> 0.16 us  [sweep_body(): dinv[:, :, index]]
    unnamed x37 -> x29, local copies, waits for them, and re-layouts: 2.63 us -> 2.61 us
  transfers between devices with their start and end apart: 4 -> 4, of which waited for: 3 -> 3; matrix products, arithmetic and copies ran while one was open for 20% -> 19% of each run, Pallas kernels for 4% -> 4%
where the time goes in v7:
time: 109 us; the launch traced here: 108 us
  waiting for transfers between devices  39 us (36%)
  local copies, waits for them, and re-layouts  20.9 us (19%)
  starting transfers between devices  19.9 us (18%)
  between operations  14 us (13%)
  Pallas kernels  9.1 us (8%)
  other arithmetic  5.62 us (5%)
    all_to_all x1, waiting for transfers between devices, sweep_body(): every = lax.all_to_all(spread, 'slab', 0, 0, tiled=True)  20.6 us
    all_to_all x1, starting transfers between devices, sweep_body(): lax.all_to_all(request, ('slab', 'cross'), split_axis=1, concat_axis=1, t...  11.2 us
    all_to_all x1, waiting for transfers between devices, sweep_body(): lax.all_to_all(answer, ('slab', 'cross'), split_axis=1, concat_axis=1, ti...  9.39 us
    all_to_all x1, waiting for transfers between devices, sweep_body(): lax.all_to_all(request, ('slab', 'cross'), split_axis=1, concat_axis=1, t...  8.99 us
    pallas_call x1, Pallas kernels, interpolate_at_owner(): pl.pallas_call(owner_kernel, out_shape=jax.ShapeDtypeStruct((rows, reques...  4.79 us
    all_to_all x1, starting transfers between devices, sweep_body(): lax.all_to_all(answer, ('slab', 'cross'), split_axis=1, concat_axis=1, ti...  4.73 us
    pallas_call x1, Pallas kernels, fold_entries(): pl.pallas_call(fold_kernel, out_shape=jax.ShapeDtypeStruct((2, width, sub...  4.31 us
    all_to_all x1, starting transfers between devices, sweep_body(): every = lax.all_to_all(spread, 'slab', 0, 0, tiled=True)  3.95 us
  transfers between devices with their start and end apart: 4, of which 3 were waited for; matrix products, arithmetic and copies ran while one was open for 19% of the time, Pallas kernels for 4%

profile of v7, /device:TPU:0, one launch (start us, length us, event | category | flops | bytes accessed | tf_op | source)
XLA Modules:
  0.0 108.4 jit_solution(224605659333269037)
XLA Ops:
  6.5 1.1 %reshape.228 = f32[5,5,2,8,128]{4,3,2,1,0:T(8,128)S(1)} reshape(f32[5,5,2,1024]{3,2,1,0:T(2,128)} %param.13) | data formatting | bytes 409600 | tf_op jit(solution)/shard_map/reshape | solution.py:148
  7.7 1.1 %reshape.227 = f32[5,5,2,8,128]{4,3,2,1,0:T(8,128)S(1)} reshape(f32[5,5,2,1024]{3,2,1,0:T(2,128)} %param.12) | data formatting | bytes 409600 | tf_op jit(solution)/shard_map/reshape | solution.py:147
  8.8 1.1 %reshape.230 = f32[5,5,2,8,128]{4,3,2,1,0:T(8,128)S(1)} reshape(f32[5,5,2,1024]{3,2,1,0:T(2,128)} %param.14) | data formatting | bytes 409600 | tf_op jit(solution)/shard_map/reshape | solution.py:149
  10.3 0.8 pad_maximum_fusion
  11.2 0.2 fusion.3
  11.8 0.4 fusion.2
  12.3 3.6 %scatter_custom_fusion = f32[16,4096]{0,1:T(8,128)S(1)} fusion(s32[1024]{0:T(1024)S(1)} %bitcast.185, f32[1024,16]{1,0:T(8,128)S(1)} %copy.68, f32[]{:T(128)} %constant.38.clone.1), kind=kCustom, calls=%fused_computation.2 | custom fusion | bytes 262148 | tf_op jit(solution)/shard_map/scatter | solution.py:180
  15.9 0.6 copy.69
  16.5 1.2 %reshape.253 = f32[128,1,512]{2,1,0:T(1,128)} reshape(f32[128,16,32]{2,1,0:T(8,128)S(1)} %bitcast.168) | data formatting | bytes 524288
  17.7 11.2 %all-to-all-start = ((f32[128,1,512]{2,1,0:T(1,128)}), f32[128,1,512]{2,1,0:T(1,128)S(1)}, u32[]{:S(2)}, u32[]{:S(2)}) async-start(f32[128,1,512]{2,1,0:T(1,128)} %reshape.253), calls=%async_computation | async-start | bytes 524288 | tf_op jit(solution)/shard_map/all_to_all | solution.py:181
  29.6 0.6 pad_bitcast_fusion.table_ref
  30.5 9.0 %all-to-all-done = f32[128,1,512]{2,1,0:T(1,128)S(1)} async-done(((f32[128,1,512]{2,1,0:T(1,128)}), f32[128,1,512]{2,1,0:T(1,128)S(1)}, u32[]{:S(2)}, u32[]{:S(2)}) %all-to-all-start) | async-done | bytes 262176 | tf_op jit(solution)/shard_map/all_to_all | solution.py:181
  39.5 0.5 broadcast.95
  40.0 1.3 %reduce.2 = f32[128,512]{1,0:T(8,128)S(1)} reduce(f32[128,1,512]{2,1,0:T(1,128)S(1)} %all-to-all-done, f32[]{:T(128)} %broadcast.95), dimensions={1}, to_apply=%all_to_all.9.reduce_sub_computation | reduce | bytes 524292 | tf_op jit(solution)/shard_map/all_to_all | solution.py:181
  41.3 0.3 reshape.254
  41.6 0.3 copy.70
  41.9 1.2 %reshape.222.request_ref = f32[16,4096]{1,0:T(8,128)} reshape(f32[16,128,32]{2,1,0:T(8,128)S(1)} %copy.70) | data formatting | bytes 524288 | tf_op jit(solution)/shard_map/reshape | solution.py:182
  43.1 4.8 %shard_map.100 = f32[8,4096]{1,0:T(8,128)} custom-call(f32[16,4096]{1,0:T(8,128)} %reshape.222.request_ref, f32[128,128]{1,0:T(8,128)} %pad_bitcast_fusion.table_ref), custom_call_target="tpu_custom_call" | custom-call | tf_op jit(solution)/shard_map/pallas_call | solution.py:50
  47.9 1.0 reshape.224
  48.9 0.2 copy.179
  49.1 0.9 reshape.255
  50.0 4.7 %all-to-all-start.1 = ((f32[128,1,160]{2,1,0:T(1,128)}), f32[128,1,160]{2,1,0:T(1,128)S(1)}, u32[]{:S(2)}, u32[]{:S(2)}) async-start(f32[128,1,160]{2,1,0:T(1,128)} %reshape.255), calls=%async_computation.1 | async-start | bytes 262144 | tf_op jit(solution)/shard_map/all_to_all | solution.py:184
  54.9 9.4 %all-to-all-done.1 = f32[128,1,160]{2,1,0:T(1,128)S(1)} async-done(((f32[128,1,160]{2,1,0:T(1,128)}), f32[128,1,160]{2,1,0:T(1,128)S(1)}, u32[]{:S(2)}, u32[]{:S(2)}) %all-to-all-start.1) | async-done | bytes 81952 | tf_op jit(solution)/shard_map/all_to_all | solution.py:184
  64.2 1.0 reduce.3
  65.4 0.8 copy.73
  66.2 2.8 %gather_fusion = f32[1024,5]{1,0:T(8,128)S(1)} fusion(f32[5,4096]{0,1:T(8,128)S(1)} %bitcast.170, s32[1024]{0:T(1024)S(1)} %broadcast_clamp_fusion), kind=kCustom, calls=%fused_computation | custom fusion | bytes 45056 | tf_op jit(solution)/shard_map/jit(_take)/gather | solution.py:185
  69.0 0.2 broadcast_select_fusion
  70.2 1.2 %broadcast_in_dim.92 = f32[32,2,5,8,128]{4,3,2,1,0:T(8,128)} broadcast(f32[2,5,8,128]{3,2,1,0:T(8,128)S(1)} %maximum_bitcast_fusion.1), dimensions={1,2,3,4} | broadcast | bytes 1351680 | tf_op jit(solution)/shard_map/broadcast_in_dim | solution.py:213
  71.4 4.0 %all-to-all-start.2 = ((f32[32,2,5,8,128]{4,3,2,1,0:T(8,128)}), f32[32,2,5,8,128]{4,3,2,1,0:T(8,128)S(1)}, u32[]{:S(2)}, u32[]{:S(2)}) async-start(f32[32,2,5,8,128]{4,3,2,1,0:T(8,128)} %broadcast_in_dim.92), calls=%async_computation.2 | async-start | bytes 2621440 | tf_op jit(solution)/shard_map/all_to_all | solution.py:214
  75.4 20.6 %all-to-all-done.2 = f32[32,2,5,8,128]{4,3,2,1,0:T(8,128)S(1)} async-done(((f32[32,2,5,8,128]{4,3,2,1,0:T(8,128)}), f32[32,2,5,8,128]{4,3,2,1,0:T(8,128)S(1)}, u32[]{:S(2)}, u32[]{:S(2)}) %all-to-all-start.2) | async-done | bytes 1310752 | tf_op jit(solution)/shard_map/all_to_all | solution.py:214
  95.9 4.3 %shard_map.101 = f32[2,5,8,128]{3,2,1,0:T(8,128)S(1)} custom-call(s32[1]{0:T(128)} %bitcast.17.index_ref, f32[32,75,8,128]{3,2,1,0:T(8,128)} %bitcast.166, f32[32,10,8,128]{3,2,1,0:T(8,128)S(1)} %bitcast.165), custom_call_target="tpu_custom_call" | custom-call | tf_op jit(solution)/shard_map/pallas_call | solution.py:115
  100.9 0.7 copy.80
  (88 shorter events, 3.6 us)
Async XLA Ops:
  6.5 89.4 %all-gather.3.cloned.1.call-start = ((), (), s32[]{:S(2)}) async-start(), calls=%async_computation.3 | async-start | bytes 10137600 | tf_op jit(solution)/shard_map/all_gather | solution.py:170
  8.8 2.3 %copy-start.5 = (s32[1024,1]{0,1:T(1,128)S(1)}, s32[1024,1]{0,1:T(1,128)}, u32[]{:S(2)}) copy-start(s32[1024,1]{0,1:T(1,128)} %param.15) | copy-start | bytes 12292
  10.2 1.4 %copy-start.8 = (s32[1024]{0:T(1024)S(1)}, s32[1024]{0:T(1024)}, u32[]{:S(2)}) copy-start(s32[1024]{0:T(1024)} %param.16) | copy-start | bytes 12292
  10.2 1.4 %copy-start.6 = (s32[8,1024]{1,0:T(8,128)S(1)}, s32[8,1024]{1,0:T(8,128)}, u32[]{:S(2)}) copy-start(s32[8,1024]{1,0:T(8,128)} %param.17) | copy-start | bytes 98308
  10.2 1.4 %copy-start.7 = (f32[8,1024]{1,0:T(8,128)S(1)}, f32[8,1024]{1,0:T(8,128)}, u32[]{:S(2)}) copy-start(f32[8,1024]{1,0:T(8,128)} %param.18) | copy-start | bytes 98308
  15.9 13.0 %copy-start.3 = (f32[5,2,1024]{2,1,0:T(2,128)S(1)}, f32[5,2,1024]{2,1,0:T(2,128)}, u32[]{:S(2)}) copy-start(f32[5,2,1024]{2,1,0:T(2,128)} %param.10) | copy-start | bytes 122884
  15.9 13.1 %copy-start.9 = (s32[1,16]{1,0:T(1,128)S(1)}, s32[1,16]{1,0:T(1,128)}, u32[]{:S(2)}) copy-start(s32[1,16]{1,0:T(1,128)} %param.19) | copy-start | bytes 196
  15.9 13.2 %copy-start = (f32[5,5,2,1024]{3,2,1,0:T(2,128)S(1)}, f32[5,5,2,1024]{3,2,1,0:T(2,128)}, u32[]{:S(2)}) copy-start(f32[5,5,2,1024]{3,2,1,0:T(2,128)} %param.13) | copy-start | bytes 614404
  16.5 12.9 %copy-start.1 = (f32[5,5,2,1024]{3,2,1,0:T(2,128)S(1)}, f32[5,5,2,1024]{3,2,1,0:T(2,128)}, u32[]{:S(2)}) copy-start(f32[5,5,2,1024]{3,2,1,0:T(2,128)} %param.12) | copy-start | bytes 614404
  16.5 13.8 %copy-start.2 = (f32[5,5,2,1024]{3,2,1,0:T(2,128)S(1)}, f32[5,5,2,1024]{3,2,1,0:T(2,128)}, u32[]{:S(2)}) copy-start(f32[5,5,2,1024]{3,2,1,0:T(2,128)} %param.14) | copy-start | bytes 614404
  17.7 21.8 %all-to-all-start = ((f32[128,1,512]{2,1,0:T(1,128)}), f32[128,1,512]{2,1,0:T(1,128)S(1)}, u32[]{:S(2)}, u32[]{:S(2)}) async-start(f32[128,1,512]{2,1,0:T(1,128)} %reshape.253), calls=%async_computation | async-start | bytes 524288 | tf_op jit(solution)/shard_map/all_to_all | solution.py:181
  50.0 14.2 %all-to-all-start.1 = ((f32[128,1,160]{2,1,0:T(1,128)}), f32[128,1,160]{2,1,0:T(1,128)S(1)}, u32[]{:S(2)}, u32[]{:S(2)}) async-start(f32[128,1,160]{2,1,0:T(1,128)} %reshape.255), calls=%async_computation.1 | async-start | bytes 262144 | tf_op jit(solution)/shard_map/all_to_all | solution.py:184
  65.3 4.3 %copy-start.4 = (f32[5,2,1024]{2,1,0:T(2,128)S(1)}, f32[5,2,1024]{2,1,0:T(2,128)}, u32[]{:S(2)}) copy-start(f32[5,2,1024]{2,1,0:T(2,128)} %param.11) | copy-start | bytes 122884
  71.4 24.5 %all-to-all-start.2 = ((f32[32,2,5,8,128]{4,3,2,1,0:T(8,128)}), f32[32,2,5,8,128]{4,3,2,1,0:T(8,128)S(1)}, u32[]{:S(2)}, u32[]{:S(2)}) async-start(f32[32,2,5,8,128]{4,3,2,1,0:T(8,128)} %broadcast_in_dim.92), calls=%async_computation.2 | async-start | bytes 2621440 | tf_op jit(solution)/shard_map/all_to_all | solution.py:214
Sparse Core Ops, SparseCore 0:
  11.2 62.8 all-gather.2

commit v8 on v7

--- a/solution.py
+++ b/solution.py
@@ -6,7 +6,6 @@
 from jax.sharding import PartitionSpec as P
 
 BLOCK_CELLS = 128
-HIGHEST = lax.Precision.HIGHEST
 
 
 def apply_block(matrix, vector):
@@ -33,7 +32,9 @@
         for k in range(1, corners):
             offs = wanted[k : k + 1] - block * BLOCK_CELLS
             spread = spread + jnp.where(offs == lanes, wts[k : k + 1], 0.0)
-        every = jnp.dot(table, spread, precision=HIGHEST, preferred_element_type=jnp.float32)
+        every = jnp.dot(
+            table, spread, precision=lax.Precision.HIGH, preferred_element_type=jnp.float32
+        )
         total = jnp.where(block == 0.0, every[0:rows], 0.0)
         for at in range(1, blocks):
             total = total + jnp.where(block == float(at), every[at * rows : (at + 1) * rows], 0.0)

time: 109 us -> 108 us (level)
  no operation moved by 1% of the time
where the time goes in v8:
time: 108 us
  waiting for transfers between devices  38.8 us (36%)
  local copies, waits for them, and re-layouts  20.9 us (19%)
  starting transfers between devices  19.9 us (18%)
  between operations  14 us (13%)
  Pallas kernels  8.49 us (8%)
  other arithmetic  5.62 us (5%)
    all_to_all x1, waiting for transfers between devices, sweep_body(): every = lax.all_to_all(spread, 'slab', 0, 0, tiled=True)  20.6 us
    all_to_all x1, starting transfers between devices, sweep_body(): lax.all_to_all(request, ('slab', 'cross'), split_axis=1, concat_axis=1, t...  11.2 us
    all_to_all x1, waiting for transfers between devices, sweep_body(): lax.all_to_all(answer, ('slab', 'cross'), split_axis=1, concat_axis=1, ti...  9.22 us
    all_to_all x1, waiting for transfers between devices, sweep_body(): lax.all_to_all(request, ('slab', 'cross'), split_axis=1, concat_axis=1, t...  8.99 us
    all_to_all x1, starting transfers between devices, sweep_body(): lax.all_to_all(answer, ('slab', 'cross'), split_axis=1, concat_axis=1, ti...  4.74 us
    pallas_call x1, Pallas kernels, fold_entries(): pl.pallas_call(fold_kernel, out_shape=jax.ShapeDtypeStruct((2, width, sub...  4.31 us
    pallas_call x1, Pallas kernels, interpolate_at_owner(): pl.pallas_call(owner_kernel, out_shape=jax.ShapeDtypeStruct((rows, reques...  4.18 us
    all_to_all x1, starting transfers between devices, sweep_body(): every = lax.all_to_all(spread, 'slab', 0, 0, tiled=True)  3.97 us
  transfers between devices with their start and end apart: 4, of which 3 were waited for; matrix products, arithmetic and copies ran while one was open for 19% of the time, Pallas kernels for 4%

profile of v8, /device:TPU:0, one launch (start us, length us, event | category | flops | bytes accessed | tf_op | source)
XLA Modules:
  0.0 107.7 jit_solution(16379448380069608673)
XLA Ops:
  6.5 1.1 %reshape.228 = f32[5,5,2,8,128]{4,3,2,1,0:T(8,128)S(1)} reshape(f32[5,5,2,1024]{3,2,1,0:T(2,128)} %param.13) | data formatting | bytes 409600 | tf_op jit(solution)/shard_map/reshape | solution.py:149
  7.7 1.1 %reshape.227 = f32[5,5,2,8,128]{4,3,2,1,0:T(8,128)S(1)} reshape(f32[5,5,2,1024]{3,2,1,0:T(2,128)} %param.12) | data formatting | bytes 409600 | tf_op jit(solution)/shard_map/reshape | solution.py:148
  8.8 1.1 %reshape.230 = f32[5,5,2,8,128]{4,3,2,1,0:T(8,128)S(1)} reshape(f32[5,5,2,1024]{3,2,1,0:T(2,128)} %param.14) | data formatting | bytes 409600 | tf_op jit(solution)/shard_map/reshape | solution.py:150
  10.3 0.8 pad_maximum_fusion
  11.2 0.2 fusion.3
  11.8 0.4 fusion.2
  12.3 3.6 %scatter_custom_fusion = f32[16,4096]{0,1:T(8,128)S(1)} fusion(s32[1024]{0:T(1024)S(1)} %bitcast.185, f32[1024,16]{1,0:T(8,128)S(1)} %copy.68, f32[]{:T(128)} %constant.38.clone.1), kind=kCustom, calls=%fused_computation.2 | custom fusion | bytes 262148 | tf_op jit(solution)/shard_map/scatter | solution.py:181
  15.9 0.6 copy.69
  16.5 1.2 %reshape.253 = f32[128,1,512]{2,1,0:T(1,128)} reshape(f32[128,16,32]{2,1,0:T(8,128)S(1)} %bitcast.168) | data formatting | bytes 524288
  17.7 11.2 %all-to-all-start = ((f32[128,1,512]{2,1,0:T(1,128)}), f32[128,1,512]{2,1,0:T(1,128)S(1)}, u32[]{:S(2)}, u32[]{:S(2)}) async-start(f32[128,1,512]{2,1,0:T(1,128)} %reshape.253), calls=%async_computation | async-start | bytes 524288 | tf_op jit(solution)/shard_map/all_to_all | solution.py:182
  29.6 0.6 pad_bitcast_fusion.table_ref
  30.5 9.0 %all-to-all-done = f32[128,1,512]{2,1,0:T(1,128)S(1)} async-done(((f32[128,1,512]{2,1,0:T(1,128)}), f32[128,1,512]{2,1,0:T(1,128)S(1)}, u32[]{:S(2)}, u32[]{:S(2)}) %all-to-all-start) | async-done | bytes 262176 | tf_op jit(solution)/shard_map/all_to_all | solution.py:182
  39.5 0.5 broadcast.95
  40.0 1.3 %reduce.2 = f32[128,512]{1,0:T(8,128)S(1)} reduce(f32[128,1,512]{2,1,0:T(1,128)S(1)} %all-to-all-done, f32[]{:T(128)} %broadcast.95), dimensions={1}, to_apply=%all_to_all.9.reduce_sub_computation | reduce | bytes 524292 | tf_op jit(solution)/shard_map/all_to_all | solution.py:182
  41.3 0.3 reshape.254
  41.6 0.3 copy.70
  41.9 1.2 %reshape.222.request_ref = f32[16,4096]{1,0:T(8,128)} reshape(f32[16,128,32]{2,1,0:T(8,128)S(1)} %copy.70) | data formatting | bytes 524288 | tf_op jit(solution)/shard_map/reshape | solution.py:183
  43.1 4.2 %shard_map.100 = f32[8,4096]{1,0:T(8,128)} custom-call(f32[16,4096]{1,0:T(8,128)} %reshape.222.request_ref, f32[128,128]{1,0:T(8,128)} %pad_bitcast_fusion.table_ref), custom_call_target="tpu_custom_call" | custom-call | tf_op jit(solution)/shard_map/pallas_call | solution.py:51
  47.3 1.1 %reshape.224 = f32[5,128,32]{2,1,0:T(8,128)S(1)} reshape(f32[5,4096]{1,0:T(8,128)} %bitcast.175) | data formatting | bytes 163840 | tf_op jit(solution)/shard_map/reshape | solution.py:184
  48.4 0.2 copy.179
  48.6 0.9 reshape.255
  49.5 4.7 %all-to-all-start.1 = ((f32[128,1,160]{2,1,0:T(1,128)}), f32[128,1,160]{2,1,0:T(1,128)S(1)}, u32[]{:S(2)}, u32[]{:S(2)}) async-start(f32[128,1,160]{2,1,0:T(1,128)} %reshape.255), calls=%async_computation.1 | async-start | bytes 262144 | tf_op jit(solution)/shard_map/all_to_all | solution.py:185
  54.3 9.2 %all-to-all-done.1 = f32[128,1,160]{2,1,0:T(1,128)S(1)} async-done(((f32[128,1,160]{2,1,0:T(1,128)}), f32[128,1,160]{2,1,0:T(1,128)S(1)}, u32[]{:S(2)}, u32[]{:S(2)}) %all-to-all-start.1) | async-done | bytes 81952 | tf_op jit(solution)/shard_map/all_to_all | solution.py:185
  63.5 1.0 reduce.3
  64.6 0.8 copy.73
  65.5 2.8 %gather_fusion = f32[1024,5]{1,0:T(8,128)S(1)} fusion(f32[5,4096]{0,1:T(8,128)S(1)} %bitcast.170, s32[1024]{0:T(1024)S(1)} %broadcast_clamp_fusion), kind=kCustom, calls=%fused_computation | custom fusion | bytes 45056 | tf_op jit(solution)/shard_map/jit(_take)/gather | solution.py:186
  68.3 0.2 broadcast_select_fusion
  69.5 1.2 %broadcast_in_dim.92 = f32[32,2,5,8,128]{4,3,2,1,0:T(8,128)} broadcast(f32[2,5,8,128]{3,2,1,0:T(8,128)S(1)} %maximum_bitcast_fusion.1), dimensions={1,2,3,4} | broadcast | bytes 1351680 | tf_op jit(solution)/shard_map/broadcast_in_dim | solution.py:214
  70.7 4.0 %all-to-all-start.2 = ((f32[32,2,5,8,128]{4,3,2,1,0:T(8,128)}), f32[32,2,5,8,128]{4,3,2,1,0:T(8,128)S(1)}, u32[]{:S(2)}, u32[]{:S(2)}) async-start(f32[32,2,5,8,128]{4,3,2,1,0:T(8,128)} %broadcast_in_dim.92), calls=%async_computation.2 | async-start | bytes 2621440 | tf_op jit(solution)/shard_map/all_to_all | solution.py:215
  74.7 20.6 %all-to-all-done.2 = f32[32,2,5,8,128]{4,3,2,1,0:T(8,128)S(1)} async-done(((f32[32,2,5,8,128]{4,3,2,1,0:T(8,128)}), f32[32,2,5,8,128]{4,3,2,1,0:T(8,128)S(1)}, u32[]{:S(2)}, u32[]{:S(2)}) %all-to-all-start.2) | async-done | bytes 1310752 | tf_op jit(solution)/shard_map/all_to_all | solution.py:215
  95.2 4.3 %shard_map.101 = f32[2,5,8,128]{3,2,1,0:T(8,128)S(1)} custom-call(s32[1]{0:T(128)} %bitcast.17.index_ref, f32[32,75,8,128]{3,2,1,0:T(8,128)} %bitcast.166, f32[32,10,8,128]{3,2,1,0:T(8,128)S(1)} %bitcast.165), custom_call_target="tpu_custom_call" | custom-call | tf_op jit(solution)/shard_map/pallas_call | solution.py:116
  100.2 0.7 copy.80
  (88 shorter events, 3.6 us)
Async XLA Ops:
  6.5 88.7 %all-gather.3.cloned.1.call-start = ((), (), s32[]{:S(2)}) async-start(), calls=%async_computation.3 | async-start | bytes 10137600 | tf_op jit(solution)/shard_map/all_gather | solution.py:171
  8.8 2.3 %copy-start.5 = (s32[1024,1]{0,1:T(1,128)S(1)}, s32[1024,1]{0,1:T(1,128)}, u32[]{:S(2)}) copy-start(s32[1024,1]{0,1:T(1,128)} %param.15) | copy-start | bytes 12292
  10.2 1.4 %copy-start.8 = (s32[1024]{0:T(1024)S(1)}, s32[1024]{0:T(1024)}, u32[]{:S(2)}) copy-start(s32[1024]{0:T(1024)} %param.16) | copy-start | bytes 12292
  10.2 1.4 %copy-start.6 = (s32[8,1024]{1,0:T(8,128)S(1)}, s32[8,1024]{1,0:T(8,128)}, u32[]{:S(2)}) copy-start(s32[8,1024]{1,0:T(8,128)} %param.17) | copy-start | bytes 98308
  10.2 1.4 %copy-start.7 = (f32[8,1024]{1,0:T(8,128)S(1)}, f32[8,1024]{1,0:T(8,128)}, u32[]{:S(2)}) copy-start(f32[8,1024]{1,0:T(8,128)} %param.18) | copy-start | bytes 98308
  15.9 13.0 %copy-start.3 = (f32[5,2,1024]{2,1,0:T(2,128)S(1)}, f32[5,2,1024]{2,1,0:T(2,128)}, u32[]{:S(2)}) copy-start(f32[5,2,1024]{2,1,0:T(2,128)} %param.10) | copy-start | bytes 122884
  15.9 13.1 %copy-start.9 = (s32[1,16]{1,0:T(1,128)S(1)}, s32[1,16]{1,0:T(1,128)}, u32[]{:S(2)}) copy-start(s32[1,16]{1,0:T(1,128)} %param.19) | copy-start | bytes 196
  15.9 13.2 %copy-start = (f32[5,5,2,1024]{3,2,1,0:T(2,128)S(1)}, f32[5,5,2,1024]{3,2,1,0:T(2,128)}, u32[]{:S(2)}) copy-start(f32[5,5,2,1024]{3,2,1,0:T(2,128)} %param.13) | copy-start | bytes 614404
  16.5 12.9 %copy-start.1 = (f32[5,5,2,1024]{3,2,1,0:T(2,128)S(1)}, f32[5,5,2,1024]{3,2,1,0:T(2,128)}, u32[]{:S(2)}) copy-start(f32[5,5,2,1024]{3,2,1,0:T(2,128)} %param.12) | copy-start | bytes 614404
  16.5 13.8 %copy-start.2 = (f32[5,5,2,1024]{3,2,1,0:T(2,128)S(1)}, f32[5,5,2,1024]{3,2,1,0:T(2,128)}, u32[]{:S(2)}) copy-start(f32[5,5,2,1024]{3,2,1,0:T(2,128)} %param.14) | copy-start | bytes 614404
  17.7 21.8 %all-to-all-start = ((f32[128,1,512]{2,1,0:T(1,128)}), f32[128,1,512]{2,1,0:T(1,128)S(1)}, u32[]{:S(2)}, u32[]{:S(2)}) async-start(f32[128,1,512]{2,1,0:T(1,128)} %reshape.253), calls=%async_computation | async-start | bytes 524288 | tf_op jit(solution)/shard_map/all_to_all | solution.py:182
  49.5 14.0 %all-to-all-start.1 = ((f32[128,1,160]{2,1,0:T(1,128)}), f32[128,1,160]{2,1,0:T(1,128)S(1)}, u32[]{:S(2)}, u32[]{:S(2)}) async-start(f32[128,1,160]{2,1,0:T(1,128)} %reshape.255), calls=%async_computation.1 | async-start | bytes 262144 | tf_op jit(solution)/shard_map/all_to_all | solution.py:185
  64.6 4.3 %copy-start.4 = (f32[5,2,1024]{2,1,0:T(2,128)S(1)}, f32[5,2,1024]{2,1,0:T(2,128)}, u32[]{:S(2)}) copy-start(f32[5,2,1024]{2,1,0:T(2,128)} %param.11) | copy-start | bytes 122884
  70.7 24.5 %all-to-all-start.2 = ((f32[32,2,5,8,128]{4,3,2,1,0:T(8,128)}), f32[32,2,5,8,128]{4,3,2,1,0:T(8,128)S(1)}, u32[]{:S(2)}, u32[]{:S(2)}) async-start(f32[32,2,5,8,128]{4,3,2,1,0:T(8,128)} %broadcast_in_dim.92), calls=%async_computation.2 | async-start | bytes 2621440 | tf_op jit(solution)/shard_map/all_to_all | solution.py:215
Sparse Core Ops, SparseCore 0:
  11.2 62.8 all-gather.2

commit v9 on v8

--- a/solution.py
+++ b/solution.py
@@ -73,10 +73,11 @@
     def matvec(at, base, vector):
         rows = []
         for i in range(width):
-            total = maps_ref[at, base + i * width] * vector[0]
-            for j in range(1, width):
-                total = total + maps_ref[at, base + i * width + j] * vector[j]
-            rows.append(total)
+            terms = [maps_ref[at, base + i * width + j] * vector[j] for j in range(width)]
+            while len(terms) > 1:
+                paired = [terms[k] + terms[k + 1] for k in range(0, len(terms) - 1, 2)]
+                terms = paired + terms[len(paired) * 2 :]
+            rows.append(terms[0])
         return rows
 
     def lower_step(at, carry):
@@ -178,12 +179,17 @@
     cells_wanted = donor_block[None, :] * BLOCK_CELLS + offsets
     payload = jnp.concatenate([cells_wanted.astype(jnp.float32), weights], axis=0)
     request = jnp.zeros((payload.shape[0], devices * capacity), jnp.float32)
-    request = request.at[:, flat_slot].set(payload).reshape(-1, devices, capacity)
+    request = request.at[:, flat_slot].set(
+        payload, unique_indices=True, mode="promise_in_bounds"
+    )
+    request = request.reshape(-1, devices, capacity)
     received = lax.all_to_all(request, ("slab", "cross"), split_axis=1, concat_axis=1, tiled=True)
     answer = interpolate_at_owner(state_flat, received.reshape(received.shape[0], -1))
     answer = answer.reshape(width, devices, capacity)
     arrived = lax.all_to_all(answer, ("slab", "cross"), split_axis=1, concat_axis=1, tiled=True)
-    interp = jnp.take(arrived.reshape(width, devices * capacity), flat_slot, axis=1)
+    interp = arrived.reshape(width, devices * capacity).at[:, flat_slot].get(
+        mode="promise_in_bounds", unique_indices=True
+    )
 
     fringe_blocks = fringe_rows // BLOCK_CELLS
     chosen = receptor_perm[0, :fringe_blocks]

time: 108 us -> 108 us (level)
  no operation moved by 1% of the time
where the time goes in v9:
time: 108 us
  waiting for transfers between devices  38.8 us (36%)
  local copies, waits for them, and re-layouts  20.9 us (19%)
  starting transfers between devices  19.9 us (18%)
  between operations  14 us (13%)
  Pallas kernels  8.49 us (8%)
  other arithmetic  5.4 us (5%)
    all_to_all x1, waiting for transfers between devices, sweep_body(): every = lax.all_to_all(spread, 'slab', 0, 0, tiled=True)  20.6 us
    all_to_all x1, starting transfers between devices, sweep_body(): lax.all_to_all(request, ('slab', 'cross'), split_axis=1, concat_axis=1, t...  11.2 us
    all_to_all x1, waiting for transfers between devices, sweep_body(): lax.all_to_all(answer, ('slab', 'cross'), split_axis=1, concat_axis=1, ti...  9.22 us
    all_to_all x1, waiting for transfers between devices, sweep_body(): lax.all_to_all(request, ('slab', 'cross'), split_axis=1, concat_axis=1, t...  8.99 us
    all_to_all x1, starting transfers between devices, sweep_body(): lax.all_to_all(answer, ('slab', 'cross'), split_axis=1, concat_axis=1, ti...  4.74 us
    pallas_call x1, Pallas kernels, fold_entries(): pl.pallas_call(fold_kernel, out_shape=jax.ShapeDtypeStruct((2, width, sub...  4.31 us
    pallas_call x1, Pallas kernels, interpolate_at_owner(): pl.pallas_call(owner_kernel, out_shape=jax.ShapeDtypeStruct((rows, reques...  4.18 us
    all_to_all x1, starting transfers between devices, sweep_body(): every = lax.all_to_all(spread, 'slab', 0, 0, tiled=True)  3.95 us
  transfers between devices with their start and end apart: 4, of which 3 were waited for; matrix products, arithmetic and copies ran while one was open for 19% of the time, Pallas kernels for 4%

profile of v9, /device:TPU:0, one launch (start us, length us, event | category | flops | bytes accessed | tf_op | source)
XLA Modules:
  0.0 107.5 jit_solution(1016787306476296528)
XLA Ops:
  6.5 1.1 %reshape.212 = f32[5,5,2,8,128]{4,3,2,1,0:T(8,128)S(1)} reshape(f32[5,5,2,1024]{3,2,1,0:T(2,128)} %param.13) | data formatting | bytes 409600 | tf_op jit(solution)/shard_map/reshape | solution.py:150
  7.7 1.1 %reshape.211 = f32[5,5,2,8,128]{4,3,2,1,0:T(8,128)S(1)} reshape(f32[5,5,2,1024]{3,2,1,0:T(2,128)} %param.12) | data formatting | bytes 409600 | tf_op jit(solution)/shard_map/reshape | solution.py:149
  8.8 1.1 %reshape.214 = f32[5,5,2,8,128]{4,3,2,1,0:T(8,128)S(1)} reshape(f32[5,5,2,1024]{3,2,1,0:T(2,128)} %param.14) | data formatting | bytes 409600 | tf_op jit(solution)/shard_map/reshape | solution.py:151
  10.3 0.8 pad_maximum_fusion
  11.2 0.2 fusion.3
  11.6 0.2 copy.68
  11.8 0.4 fusion.2
  12.2 3.6 %scatter_custom_fusion = f32[16,4096]{0,1:T(8,128)S(1)} fusion(s32[1024]{0:T(1024)S(1)} %bitcast.184, f32[1024,16]{1,0:T(8,128)S(1)} %copy.68, f32[]{:T(128)} %constant.10.clone.1), kind=kCustom, calls=%fused_computation.2 | custom fusion | bytes 262148 | tf_op jit(solution)/shard_map/scatter | solution.py:182
  15.9 0.6 copy.69
  16.5 1.2 %reshape.236 = f32[128,1,512]{2,1,0:T(1,128)} reshape(f32[128,16,32]{2,1,0:T(8,128)S(1)} %bitcast.167) | data formatting | bytes 524288
  17.7 11.2 %all-to-all-start = ((f32[128,1,512]{2,1,0:T(1,128)}), f32[128,1,512]{2,1,0:T(1,128)S(1)}, u32[]{:S(2)}, u32[]{:S(2)}) async-start(f32[128,1,512]{2,1,0:T(1,128)} %reshape.236), calls=%async_computation | async-start | bytes 524288 | tf_op jit(solution)/shard_map/all_to_all | solution.py:186
  29.6 0.6 pad_bitcast_fusion.table_ref
  30.5 9.0 %all-to-all-done = f32[128,1,512]{2,1,0:T(1,128)S(1)} async-done(((f32[128,1,512]{2,1,0:T(1,128)}), f32[128,1,512]{2,1,0:T(1,128)S(1)}, u32[]{:S(2)}, u32[]{:S(2)}) %all-to-all-start) | async-done | bytes 262176 | tf_op jit(solution)/shard_map/all_to_all | solution.py:186
  39.5 0.5 broadcast.86
  40.0 1.3 %reduce = f32[128,512]{1,0:T(8,128)S(1)} reduce(f32[128,1,512]{2,1,0:T(1,128)S(1)} %all-to-all-done, f32[]{:T(128)} %broadcast.86), dimensions={1}, to_apply=%all_to_all.9.reduce_sub_computation | reduce | bytes 524292 | tf_op jit(solution)/shard_map/all_to_all | solution.py:186
  41.3 0.3 reshape.237
  41.5 0.3 copy.70
  41.9 1.2 %reshape.206.request_ref = f32[16,4096]{1,0:T(8,128)} reshape(f32[16,128,32]{2,1,0:T(8,128)S(1)} %copy.70) | data formatting | bytes 524288 | tf_op jit(solution)/shard_map/reshape | solution.py:187
  43.1 4.2 %shard_map.100 = f32[8,4096]{1,0:T(8,128)} custom-call(f32[16,4096]{1,0:T(8,128)} %reshape.206.request_ref, f32[128,128]{1,0:T(8,128)} %pad_bitcast_fusion.table_ref), custom_call_target="tpu_custom_call" | custom-call | tf_op jit(solution)/shard_map/pallas_call | solution.py:51
  47.3 1.1 %reshape.208 = f32[5,128,32]{2,1,0:T(8,128)S(1)} reshape(f32[5,4096]{1,0:T(8,128)} %bitcast.174) | data formatting | bytes 163840 | tf_op jit(solution)/shard_map/reshape | solution.py:188
  48.4 0.2 copy.179
  48.6 0.9 reshape.238
  49.5 4.7 %all-to-all-start.1 = ((f32[128,1,160]{2,1,0:T(1,128)}), f32[128,1,160]{2,1,0:T(1,128)S(1)}, u32[]{:S(2)}, u32[]{:S(2)}) async-start(f32[128,1,160]{2,1,0:T(1,128)} %reshape.238), calls=%async_computation.1 | async-start | bytes 262144 | tf_op jit(solution)/shard_map/all_to_all | solution.py:189
  54.3 9.2 %all-to-all-done.1 = f32[128,1,160]{2,1,0:T(1,128)S(1)} async-done(((f32[128,1,160]{2,1,0:T(1,128)}), f32[128,1,160]{2,1,0:T(1,128)S(1)}, u32[]{:S(2)}, u32[]{:S(2)}) %all-to-all-start.1) | async-done | bytes 81952 | tf_op jit(solution)/shard_map/all_to_all | solution.py:189
  63.5 1.0 reduce.1
  64.6 0.8 copy.73
  65.5 2.8 %gather_fusion = f32[1024,5]{1,0:T(8,128)S(1)} fusion(f32[5,4096]{0,1:T(8,128)S(1)} %bitcast.169, s32[1024]{0:T(1024)S(1)} %broadcast_clamp_fusion), kind=kCustom, calls=%fused_computation | custom fusion | bytes 45056 | tf_op jit(solution)/shard_map/gather | solution.py:190
  69.3 1.2 %broadcast_in_dim.81 = f32[32,2,5,8,128]{4,3,2,1,0:T(8,128)} broadcast(f32[2,5,8,128]{3,2,1,0:T(8,128)S(1)} %maximum_bitcast_fusion.1), dimensions={1,2,3,4} | broadcast | bytes 1351680 | tf_op jit(solution)/shard_map/broadcast_in_dim | solution.py:220
  70.5 4.0 %all-to-all-start.2 = ((f32[32,2,5,8,128]{4,3,2,1,0:T(8,128)}), f32[32,2,5,8,128]{4,3,2,1,0:T(8,128)S(1)}, u32[]{:S(2)}, u32[]{:S(2)}) async-start(f32[32,2,5,8,128]{4,3,2,1,0:T(8,128)} %broadcast_in_dim.81), calls=%async_computation.2 | async-start | bytes 2621440 | tf_op jit(solution)/shard_map/all_to_all | solution.py:221
  74.4 20.6 %all-to-all-done.2 = f32[32,2,5,8,128]{4,3,2,1,0:T(8,128)S(1)} async-done(((f32[32,2,5,8,128]{4,3,2,1,0:T(8,128)}), f32[32,2,5,8,128]{4,3,2,1,0:T(8,128)S(1)}, u32[]{:S(2)}, u32[]{:S(2)}) %all-to-all-start.2) | async-done | bytes 1310752 | tf_op jit(solution)/shard_map/all_to_all | solution.py:221
  95.0 4.3 %shard_map.101 = f32[2,5,8,128]{3,2,1,0:T(8,128)S(1)} custom-call(s32[1]{0:T(128)} %bitcast.17.index_ref, f32[32,75,8,128]{3,2,1,0:T(8,128)} %bitcast.165, f32[32,10,8,128]{3,2,1,0:T(8,128)S(1)} %bitcast.164), custom_call_target="tpu_custom_call" | custom-call | tf_op jit(solution)/shard_map/pallas_call | solution.py:117
  100.0 0.7 copy.80
  (87 shorter events, 3.4 us)
Async XLA Ops:
  6.5 88.4 %all-gather.3.cloned.1.call-start = ((), (), s32[]{:S(2)}) async-start(), calls=%async_computation.3 | async-start | bytes 10137600 | tf_op jit(solution)/shard_map/all_gather | solution.py:172
  8.8 2.3 %copy-start.5 = (s32[1024,1]{0,1:T(1,128)S(1)}, s32[1024,1]{0,1:T(1,128)}, u32[]{:S(2)}) copy-start(s32[1024,1]{0,1:T(1,128)} %param.15) | copy-start | bytes 12292
  10.2 1.4 %copy-start.8 = (s32[1024]{0:T(1024)S(1)}, s32[1024]{0:T(1024)}, u32[]{:S(2)}) copy-start(s32[1024]{0:T(1024)} %param.16) | copy-start | bytes 12292
  10.2 1.4 %copy-start.6 = (s32[8,1024]{1,0:T(8,128)S(1)}, s32[8,1024]{1,0:T(8,128)}, u32[]{:S(2)}) copy-start(s32[8,1024]{1,0:T(8,128)} %param.17) | copy-start | bytes 98308
  10.2 1.4 %copy-start.7 = (f32[8,1024]{1,0:T(8,128)S(1)}, f32[8,1024]{1,0:T(8,128)}, u32[]{:S(2)}) copy-start(f32[8,1024]{1,0:T(8,128)} %param.18) | copy-start | bytes 98308
  15.8 13.0 %copy-start.3 = (f32[5,2,1024]{2,1,0:T(2,128)S(1)}, f32[5,2,1024]{2,1,0:T(2,128)}, u32[]{:S(2)}) copy-start(f32[5,2,1024]{2,1,0:T(2,128)} %param.10) | copy-start | bytes 122884
  15.9 13.1 %copy-start.9 = (s32[1,16]{1,0:T(1,128)S(1)}, s32[1,16]{1,0:T(1,128)}, u32[]{:S(2)}) copy-start(s32[1,16]{1,0:T(1,128)} %param.19) | copy-start | bytes 196
  15.9 13.2 %copy-start = (f32[5,5,2,1024]{3,2,1,0:T(2,128)S(1)}, f32[5,5,2,1024]{3,2,1,0:T(2,128)}, u32[]{:S(2)}) copy-start(f32[5,5,2,1024]{3,2,1,0:T(2,128)} %param.13) | copy-start | bytes 614404
  16.5 12.9 %copy-start.1 = (f32[5,5,2,1024]{3,2,1,0:T(2,128)S(1)}, f32[5,5,2,1024]{3,2,1,0:T(2,128)}, u32[]{:S(2)}) copy-start(f32[5,5,2,1024]{3,2,1,0:T(2,128)} %param.12) | copy-start | bytes 614404
  16.5 13.8 %copy-start.2 = (f32[5,5,2,1024]{3,2,1,0:T(2,128)S(1)}, f32[5,5,2,1024]{3,2,1,0:T(2,128)}, u32[]{:S(2)}) copy-start(f32[5,5,2,1024]{3,2,1,0:T(2,128)} %param.14) | copy-start | bytes 614404
  17.7 21.8 %all-to-all-start = ((f32[128,1,512]{2,1,0:T(1,128)}), f32[128,1,512]{2,1,0:T(1,128)S(1)}, u32[]{:S(2)}, u32[]{:S(2)}) async-start(f32[128,1,512]{2,1,0:T(1,128)} %reshape.236), calls=%async_computation | async-start | bytes 524288 | tf_op jit(solution)/shard_map/all_to_all | solution.py:186
  49.5 14.0 %all-to-all-start.1 = ((f32[128,1,160]{2,1,0:T(1,128)}), f32[128,1,160]{2,1,0:T(1,128)S(1)}, u32[]{:S(2)}, u32[]{:S(2)}) async-start(f32[128,1,160]{2,1,0:T(1,128)} %reshape.238), calls=%async_computation.1 | async-start | bytes 262144 | tf_op jit(solution)/shard_map/all_to_all | solution.py:189
  64.5 4.2 %copy-start.4 = (f32[5,2,1024]{2,1,0:T(2,128)S(1)}, f32[5,2,1024]{2,1,0:T(2,128)}, u32[]{:S(2)}) copy-start(f32[5,2,1024]{2,1,0:T(2,128)} %param.11) | copy-start | bytes 122884
  70.5 24.5 %all-to-all-start.2 = ((f32[32,2,5,8,128]{4,3,2,1,0:T(8,128)}), f32[32,2,5,8,128]{4,3,2,1,0:T(8,128)S(1)}, u32[]{:S(2)}, u32[]{:S(2)}) async-start(f32[32,2,5,8,128]{4,3,2,1,0:T(8,128)} %broadcast_in_dim.81), calls=%async_computation.2 | async-start | bytes 2621440 | tf_op jit(solution)/shard_map/all_to_all | solution.py:221
Sparse Core Ops, SparseCore 0:
  11.2 62.8 all-gather.2

commit v10 on v9

--- a/solution.py
+++ b/solution.py
@@ -20,7 +20,7 @@
     corners = request_ref.shape[0] // 2
     rows = out_ref.shape[0]
     blocks = table_ref.shape[0] // rows
-    chunk = 512
+    chunk = 256
     table = table_ref[...]
     lanes = lax.broadcasted_iota(jnp.int32, (BLOCK_CELLS, chunk), 0).astype(jnp.float32)
     for part in range(request_ref.shape[1] // chunk):
@@ -179,17 +179,12 @@
     cells_wanted = donor_block[None, :] * BLOCK_CELLS + offsets
     payload = jnp.concatenate([cells_wanted.astype(jnp.float32), weights], axis=0)
     request = jnp.zeros((payload.shape[0], devices * capacity), jnp.float32)
-    request = request.at[:, flat_slot].set(
-        payload, unique_indices=True, mode="promise_in_bounds"
-    )
-    request = request.reshape(-1, devices, capacity)
+    request = request.at[:, flat_slot].set(payload).reshape(-1, devices, capacity)
     received = lax.all_to_all(request, ("slab", "cross"), split_axis=1, concat_axis=1, tiled=True)
     answer = interpolate_at_owner(state_flat, received.reshape(received.shape[0], -1))
     answer = answer.reshape(width, devices, capacity)
     arrived = lax.all_to_all(answer, ("slab", "cross"), split_axis=1, concat_axis=1, tiled=True)
-    interp = arrived.reshape(width, devices * capacity).at[:, flat_slot].get(
-        mode="promise_in_bounds", unique_indices=True
-    )
+    interp = jnp.take(arrived.reshape(width, devices * capacity), flat_slot, axis=1)
 
     fringe_blocks = fringe_rows // BLOCK_CELLS
     chosen = receptor_perm[0, :fringe_blocks]

time: 108 us -> 108 us (level)
  no operation moved by 1% of the time
where the time goes in v10:
time: 108 us
  waiting for transfers between devices  38.8 us (36%)
  local copies, waits for them, and re-layouts  20.9 us (19%)
  starting transfers between devices  19.9 us (18%)
  between operations  14 us (13%)
  Pallas kernels  8.49 us (8%)
  other arithmetic  5.62 us (5%)
    all_to_all x1, waiting for transfers between devices, sweep_body(): every = lax.all_to_all(spread, 'slab', 0, 0, tiled=True)  20.6 us
    all_to_all x1, starting transfers between devices, sweep_body(): lax.all_to_all(request, ('slab', 'cross'), split_axis=1, concat_axis=1, t...  11.2 us
    all_to_all x1, waiting for transfers between devices, sweep_body(): lax.all_to_all(answer, ('slab', 'cross'), split_axis=1, concat_axis=1, ti...  9.22 us
    all_to_all x1, waiting for transfers between devices, sweep_body(): lax.all_to_all(request, ('slab', 'cross'), split_axis=1, concat_axis=1, t...  8.99 us
    all_to_all x1, starting transfers between devices, sweep_body(): lax.all_to_all(answer, ('slab', 'cross'), split_axis=1, concat_axis=1, ti...  4.74 us
    pallas_call x1, Pallas kernels, fold_entries(): pl.pallas_call(fold_kernel, out_shape=jax.ShapeDtypeStruct((2, width, sub...  4.31 us
    pallas_call x1, Pallas kernels, interpolate_at_owner(): pl.pallas_call(owner_kernel, out_shape=jax.ShapeDtypeStruct((rows, reques...  4.18 us
    all_to_all x1, starting transfers between devices, sweep_body(): every = lax.all_to_all(spread, 'slab', 0, 0, tiled=True)  3.97 us
  transfers between devices with their start and end apart: 4, of which 3 were waited for; matrix products, arithmetic and copies ran while one was open for 19% of the time, Pallas kernels for 4%

profile of v10, /device:TPU:0, one launch (start us, length us, event | category | flops | bytes accessed | tf_op | source)
XLA Modules:
  0.0 107.7 jit_solution(6746087355073382742)
XLA Ops:
  6.5 1.1 %reshape.228 = f32[5,5,2,8,128]{4,3,2,1,0:T(8,128)S(1)} reshape(f32[5,5,2,1024]{3,2,1,0:T(2,128)} %param.13) | data formatting | bytes 409600 | tf_op jit(solution)/shard_map/reshape | solution.py:150
  7.7 1.1 %reshape.227 = f32[5,5,2,8,128]{4,3,2,1,0:T(8,128)S(1)} reshape(f32[5,5,2,1024]{3,2,1,0:T(2,128)} %param.12) | data formatting | bytes 409600 | tf_op jit(solution)/shard_map/reshape | solution.py:149
  8.8 1.1 %reshape.230 = f32[5,5,2,8,128]{4,3,2,1,0:T(8,128)S(1)} reshape(f32[5,5,2,1024]{3,2,1,0:T(2,128)} %param.14) | data formatting | bytes 409600 | tf_op jit(solution)/shard_map/reshape | solution.py:151
  10.3 0.8 pad_maximum_fusion
  11.2 0.2 fusion.3
  11.8 0.4 fusion.2
  12.3 3.6 %scatter_custom_fusion = f32[16,4096]{0,1:T(8,128)S(1)} fusion(s32[1024]{0:T(1024)S(1)} %bitcast.185, f32[1024,16]{1,0:T(8,128)S(1)} %copy.68, f32[]{:T(128)} %constant.38.clone.1), kind=kCustom, calls=%fused_computation.2 | custom fusion | bytes 262148 | tf_op jit(solution)/shard_map/scatter | solution.py:182
  15.9 0.6 copy.69
  16.5 1.2 %reshape.253 = f32[128,1,512]{2,1,0:T(1,128)} reshape(f32[128,16,32]{2,1,0:T(8,128)S(1)} %bitcast.168) | data formatting | bytes 524288
  17.7 11.2 %all-to-all-start = ((f32[128,1,512]{2,1,0:T(1,128)}), f32[128,1,512]{2,1,0:T(1,128)S(1)}, u32[]{:S(2)}, u32[]{:S(2)}) async-start(f32[128,1,512]{2,1,0:T(1,128)} %reshape.253), calls=%async_computation | async-start | bytes 524288 | tf_op jit(solution)/shard_map/all_to_all | solution.py:183
  29.6 0.6 pad_bitcast_fusion.table_ref
  30.5 9.0 %all-to-all-done = f32[128,1,512]{2,1,0:T(1,128)S(1)} async-done(((f32[128,1,512]{2,1,0:T(1,128)}), f32[128,1,512]{2,1,0:T(1,128)S(1)}, u32[]{:S(2)}, u32[]{:S(2)}) %all-to-all-start) | async-done | bytes 262176 | tf_op jit(solution)/shard_map/all_to_all | solution.py:183
  39.5 0.5 broadcast.95
  40.0 1.3 %reduce.2 = f32[128,512]{1,0:T(8,128)S(1)} reduce(f32[128,1,512]{2,1,0:T(1,128)S(1)} %all-to-all-done, f32[]{:T(128)} %broadcast.95), dimensions={1}, to_apply=%all_to_all.9.reduce_sub_computation | reduce | bytes 524292 | tf_op jit(solution)/shard_map/all_to_all | solution.py:183
  41.3 0.3 reshape.254
  41.6 0.3 copy.70
  41.9 1.2 %reshape.222.request_ref = f32[16,4096]{1,0:T(8,128)} reshape(f32[16,128,32]{2,1,0:T(8,128)S(1)} %copy.70) | data formatting | bytes 524288 | tf_op jit(solution)/shard_map/reshape | solution.py:184
  43.1 4.2 %shard_map.100 = f32[8,4096]{1,0:T(8,128)} custom-call(f32[16,4096]{1,0:T(8,128)} %reshape.222.request_ref, f32[128,128]{1,0:T(8,128)} %pad_bitcast_fusion.table_ref), custom_call_target="tpu_custom_call" | custom-call | tf_op jit(solution)/shard_map/pallas_call | solution.py:51
  47.3 1.1 %reshape.224 = f32[5,128,32]{2,1,0:T(8,128)S(1)} reshape(f32[5,4096]{1,0:T(8,128)} %bitcast.175) | data formatting | bytes 163840 | tf_op jit(solution)/shard_map/reshape | solution.py:185
  48.4 0.2 copy.179
  48.6 0.9 reshape.255
  49.5 4.7 %all-to-all-start.1 = ((f32[128,1,160]{2,1,0:T(1,128)}), f32[128,1,160]{2,1,0:T(1,128)S(1)}, u32[]{:S(2)}, u32[]{:S(2)}) async-start(f32[128,1,160]{2,1,0:T(1,128)} %reshape.255), calls=%async_computation.1 | async-start | bytes 262144 | tf_op jit(solution)/shard_map/all_to_all | solution.py:186
  54.3 9.2 %all-to-all-done.1 = f32[128,1,160]{2,1,0:T(1,128)S(1)} async-done(((f32[128,1,160]{2,1,0:T(1,128)}), f32[128,1,160]{2,1,0:T(1,128)S(1)}, u32[]{:S(2)}, u32[]{:S(2)}) %all-to-all-start.1) | async-done | bytes 81952 | tf_op jit(solution)/shard_map/all_to_all | solution.py:186
  63.5 1.0 reduce.3
  64.6 0.8 copy.73
  65.5 2.8 %gather_fusion = f32[1024,5]{1,0:T(8,128)S(1)} fusion(f32[5,4096]{0,1:T(8,128)S(1)} %bitcast.170, s32[1024]{0:T(1024)S(1)} %broadcast_clamp_fusion), kind=kCustom, calls=%fused_computation | custom fusion | bytes 45056 | tf_op jit(solution)/shard_map/jit(_take)/gather | solution.py:187
  68.3 0.2 broadcast_select_fusion
  69.5 1.2 %broadcast_in_dim.92 = f32[32,2,5,8,128]{4,3,2,1,0:T(8,128)} broadcast(f32[2,5,8,128]{3,2,1,0:T(8,128)S(1)} %maximum_bitcast_fusion.1), dimensions={1,2,3,4} | broadcast | bytes 1351680 | tf_op jit(solution)/shard_map/broadcast_in_dim | solution.py:215
  70.7 4.0 %all-to-all-start.2 = ((f32[32,2,5,8,128]{4,3,2,1,0:T(8,128)}), f32[32,2,5,8,128]{4,3,2,1,0:T(8,128)S(1)}, u32[]{:S(2)}, u32[]{:S(2)}) async-start(f32[32,2,5,8,128]{4,3,2,1,0:T(8,128)} %broadcast_in_dim.92), calls=%async_computation.2 | async-start | bytes 2621440 | tf_op jit(solution)/shard_map/all_to_all | solution.py:216
  74.7 20.6 %all-to-all-done.2 = f32[32,2,5,8,128]{4,3,2,1,0:T(8,128)S(1)} async-done(((f32[32,2,5,8,128]{4,3,2,1,0:T(8,128)}), f32[32,2,5,8,128]{4,3,2,1,0:T(8,128)S(1)}, u32[]{:S(2)}, u32[]{:S(2)}) %all-to-all-start.2) | async-done | bytes 1310752 | tf_op jit(solution)/shard_map/all_to_all | solution.py:216
  95.2 4.3 %shard_map.101 = f32[2,5,8,128]{3,2,1,0:T(8,128)S(1)} custom-call(s32[1]{0:T(128)} %bitcast.17.index_ref, f32[32,75,8,128]{3,2,1,0:T(8,128)} %bitcast.166, f32[32,10,8,128]{3,2,1,0:T(8,128)S(1)} %bitcast.165), custom_call_target="tpu_custom_call" | custom-call | tf_op jit(solution)/shard_map/pallas_call | solution.py:117
  100.2 0.7 copy.80
  (88 shorter events, 3.6 us)
Async XLA Ops:
  6.5 88.7 %all-gather.3.cloned.1.call-start = ((), (), s32[]{:S(2)}) async-start(), calls=%async_computation.3 | async-start | bytes 10137600 | tf_op jit(solution)/shard_map/all_gather | solution.py:172
  8.8 2.3 %copy-start.5 = (s32[1024,1]{0,1:T(1,128)S(1)}, s32[1024,1]{0,1:T(1,128)}, u32[]{:S(2)}) copy-start(s32[1024,1]{0,1:T(1,128)} %param.15) | copy-start | bytes 12292
  10.2 1.4 %copy-start.8 = (s32[1024]{0:T(1024)S(1)}, s32[1024]{0:T(1024)}, u32[]{:S(2)}) copy-start(s32[1024]{0:T(1024)} %param.16) | copy-start | bytes 12292
  10.2 1.4 %copy-start.6 = (s32[8,1024]{1,0:T(8,128)S(1)}, s32[8,1024]{1,0:T(8,128)}, u32[]{:S(2)}) copy-start(s32[8,1024]{1,0:T(8,128)} %param.17) | copy-start | bytes 98308
  10.2 1.4 %copy-start.7 = (f32[8,1024]{1,0:T(8,128)S(1)}, f32[8,1024]{1,0:T(8,128)}, u32[]{:S(2)}) copy-start(f32[8,1024]{1,0:T(8,128)} %param.18) | copy-start | bytes 98308
  15.9 13.0 %copy-start.3 = (f32[5,2,1024]{2,1,0:T(2,128)S(1)}, f32[5,2,1024]{2,1,0:T(2,128)}, u32[]{:S(2)}) copy-start(f32[5,2,1024]{2,1,0:T(2,128)} %param.10) | copy-start | bytes 122884
  15.9 13.1 %copy-start.9 = (s32[1,16]{1,0:T(1,128)S(1)}, s32[1,16]{1,0:T(1,128)}, u32[]{:S(2)}) copy-start(s32[1,16]{1,0:T(1,128)} %param.19) | copy-start | bytes 196
  15.9 13.2 %copy-start = (f32[5,5,2,1024]{3,2,1,0:T(2,128)S(1)}, f32[5,5,2,1024]{3,2,1,0:T(2,128)}, u32[]{:S(2)}) copy-start(f32[5,5,2,1024]{3,2,1,0:T(2,128)} %param.13) | copy-start | bytes 614404
  16.5 12.9 %copy-start.1 = (f32[5,5,2,1024]{3,2,1,0:T(2,128)S(1)}, f32[5,5,2,1024]{3,2,1,0:T(2,128)}, u32[]{:S(2)}) copy-start(f32[5,5,2,1024]{3,2,1,0:T(2,128)} %param.12) | copy-start | bytes 614404
  16.5 13.8 %copy-start.2 = (f32[5,5,2,1024]{3,2,1,0:T(2,128)S(1)}, f32[5,5,2,1024]{3,2,1,0:T(2,128)}, u32[]{:S(2)}) copy-start(f32[5,5,2,1024]{3,2,1,0:T(2,128)} %param.14) | copy-start | bytes 614404
  17.7 21.8 %all-to-all-start = ((f32[128,1,512]{2,1,0:T(1,128)}), f32[128,1,512]{2,1,0:T(1,128)S(1)}, u32[]{:S(2)}, u32[]{:S(2)}) async-start(f32[128,1,512]{2,1,0:T(1,128)} %reshape.253), calls=%async_computation | async-start | bytes 524288 | tf_op jit(solution)/shard_map/all_to_all | solution.py:183
  49.5 14.0 %all-to-all-start.1 = ((f32[128,1,160]{2,1,0:T(1,128)}), f32[128,1,160]{2,1,0:T(1,128)S(1)}, u32[]{:S(2)}, u32[]{:S(2)}) async-start(f32[128,1,160]{2,1,0:T(1,128)} %reshape.255), calls=%async_computation.1 | async-start | bytes 262144 | tf_op jit(solution)/shard_map/all_to_all | solution.py:186
  64.6 4.3 %copy-start.4 = (f32[5,2,1024]{2,1,0:T(2,128)S(1)}, f32[5,2,1024]{2,1,0:T(2,128)}, u32[]{:S(2)}) copy-start(f32[5,2,1024]{2,1,0:T(2,128)} %param.11) | copy-start | bytes 122884
  70.7 24.5 %all-to-all-start.2 = ((f32[32,2,5,8,128]{4,3,2,1,0:T(8,128)}), f32[32,2,5,8,128]{4,3,2,1,0:T(8,128)S(1)}, u32[]{:S(2)}, u32[]{:S(2)}) async-start(f32[32,2,5,8,128]{4,3,2,1,0:T(8,128)} %broadcast_in_dim.92), calls=%async_computation.2 | async-start | bytes 2621440 | tf_op jit(solution)/shard_map/all_to_all | solution.py:216
Sparse Core Ops, SparseCore 0:
  11.2 62.8 all-gather.2
